TPU v7x, 256 devices: a whole 4x4x8 slice. The times are simulated.
256 devices in a mesh: leaf: 2 (over core), row: 8 (over z), col: 16 (over y, x).
Axes of the slice: x: 4, y: 4, z: 8, core: 2. Of those that a mesh axis runs over, the one named last changes fastest.
Arguments:
- front: float32 [2, 8, 8, 128, 4, 16, 128], P('leaf', None, 'row', None, None, 'col'), as said below
- parent: float32 [4, 2, 8, 128, 4, 16, 128], P(None, 'leaf', 'row', None, None, 'col'), may hold values from -0.2 to 0.2
- tile_map: int32 [2, 56], replicated, may hold values from 0 to 63, as said below
- col_shift: int32 [4], replicated, may hold values from 0 to 7
Outputs:
- factored: float32 [2, 8, 8, 128, 4, 16, 128], P('leaf', None, 'row', None, None, 'col')
- new_parent: float32 [4, 2, 8, 128, 4, 16, 128], P(None, 'leaf', 'row', None, None, 'col')
Inputs may be any that keep to these rules, and one draw needn't show every extreme that they name: For each leaf the 8192 x 8192 matrix read from front is symmetric positive definite. Entry [l, e] names the parent tile joined by tile 8 + e of child l; no row repeats a value. The parent tile q = tile_map[l, e] has (q mod 16 + col_shift[q // 16]) mod 16 equal to (8 + e) mod 16. Among the tiles of one child whose indices are equal mod 8, at most 1 have parent tiles equal mod 16.
All inputs are finite; a program needn't handle non-finite values.
Results may differ from a plain program's by a relative error of at most 0.0001.
Values sent between devices are 32-bit elements; how exact they have to be, the bound alone decides.
No kernel may reach another device: no remote copies, remote signals or barrier semaphores. Data moves between devices by JAX's collectives and lax.ppermute only.
A program may use at most 128 MiB of HBM per device.

v0:
```python
import jax
import jax.numpy as jnp
from jax import lax
from jax.sharding import PartitionSpec as P

TILE = 128
PB = 512
PANELS = 2
NPIV = 1024


HIGHEST = lax.Precision.HIGHEST


def spread(value, axis, source):
    kept = jnp.where(lax.axis_index(axis) == source, value, 0).astype(value.dtype)
    return lax.psum(kept, axis)


def update_slots(working, next_rows, column_factor, slot_low, slot_high):
    product = jnp.einsum(
        "atp,bsp->atbs",
        next_rows,
        column_factor,
        precision=HIGHEST,
        preferred_element_type=jnp.float32,
    )
    return working.at[:, :, slot_low:slot_high, :].add(-product)


def per_device(front, parent, tile_map, col_shift):
    leaf_count = lax.axis_size("leaf")
    row_count = lax.axis_size("row")
    col_count = lax.axis_size("col")
    leaf_index = lax.axis_index("leaf")
    row_index = lax.axis_index("row")
    col_index = lax.axis_index("col")
    local_front = front[0, :, 0, :, :, 0, :]
    row_slots = local_front.shape[0]
    col_slots = local_front.shape[2]
    panel_tiles = PB // TILE
    pivot_tiles = NPIV // TILE
    row_tiles = jnp.arange(row_slots, dtype=jnp.int32) * row_count + row_index
    col_tiles = jnp.arange(col_slots, dtype=jnp.int32) * col_count + col_index

    def fetch_panel(working, panel_index):
        pieces = []
        for offset in range(panel_tiles):
            column = panel_index * panel_tiles + offset
            column_tile = working[:, :, column // col_count, :]
            pieces.append(spread(column_tile, "col", column % col_count))
        return jnp.concatenate(pieces, axis=2)

    def write_factor(working, factor, panel_index):
        first_column = panel_index * panel_tiles
        slot_values = sorted(
            set([(first_column + offset) // col_count for offset in range(panel_tiles)])
        )
        for slot_index in slot_values:
            current = working[:, :, slot_index, :]
            for offset in range(panel_tiles):
                column = first_column + offset
                if column // col_count == slot_index:
                    current = jnp.where(
                        col_index == column % col_count,
                        factor[:, :, offset * TILE : (offset + 1) * TILE],
                        current,
                    )
            working = working.at[:, :, slot_index, :].set(current)
        return working

    working = local_front
    panel_block = fetch_panel(working, 0)
    for panel_index in range(PANELS):
        first_tile = panel_index * panel_tiles
        factor_slot_index = first_tile // row_count
        start_row = first_tile % row_count
        gathered = lax.all_gather(panel_block[factor_slot_index], "row", axis=0, tiled=True)
        diagonal_block = gathered[start_row * TILE : (start_row + panel_tiles) * TILE]
        lower_factor = jnp.linalg.cholesky(diagonal_block)
        factor_flattened = panel_block.reshape(row_slots * TILE, PB)
        solved = lax.linalg.triangular_solve(
            lower_factor, factor_flattened, left_side=False, lower=True, transpose_a=True
        )
        solved = solved.reshape(row_slots, TILE, PB)
        offset_tile = jnp.clip(row_index - start_row, 0, panel_tiles - 1)
        diagonal_rows = lax.dynamic_slice_in_dim(lower_factor, offset_tile * TILE, TILE, 0)
        in_panel = (row_tiles >= first_tile) & (row_tiles < first_tile + panel_tiles)
        factor_factor = jnp.where(in_panel[:, None, None], diagonal_rows[None], solved)
        factor_factor = jnp.where((row_tiles >= first_tile)[:, None, None], factor_factor, 0.0)
        next_rows = jnp.where(
            (row_tiles >= first_tile + panel_tiles)[:, None, None], factor_factor, 0.0
        )
        group_size = col_count // row_count
        owner_rows = spread(next_rows, "row", col_index % row_count)
        grouped = owner_rows.reshape(col_slots, group_size, TILE, PB)
        column_factor = lax.dynamic_index_in_dim(grouped, col_index // row_count, 1, keepdims=False)
        column_factor = jnp.where(
            (col_tiles >= first_tile + panel_tiles)[:, None, None], column_factor, 0.0
        )
        factor, next_rows, column_factor = (factor_factor, next_rows, column_factor)
        working = update_slots(working, next_rows, column_factor, 0, col_slots)
        upcoming = (
            fetch_panel(working, panel_index + 1) if panel_index + 1 < PANELS else panel_block
        )
        working = write_factor(working, factor, panel_index)
        panel_block = upcoming
    upper_part = (row_tiles < pivot_tiles)[:, None, None, None] & (col_tiles >= pivot_tiles)[
        None, None, :, None
    ]
    working = jnp.where(upper_part, 0.0, working)
    factored = working.reshape(front.shape)
    contribution = jnp.where((col_tiles >= pivot_tiles)[None, None, :, None], working, 0.0)
    contrib_count = tile_map.shape[1]
    entry_ids = jnp.arange(contrib_count, dtype=jnp.int32)
    own_map = lax.dynamic_index_in_dim(tile_map, leaf_index, 0, keepdims=False)
    row_match = (row_tiles - pivot_tiles)[:, None] == entry_ids[None, :]
    row_targets = jnp.sum(jnp.where(row_match, own_map[None, :], 0), axis=1)
    row_valid = row_tiles >= pivot_tiles
    owner_count = leaf_count * row_count
    destination = row_targets % owner_count
    parent_row_slot = row_targets // owner_count
    slot_ids = jnp.arange(row_slots, dtype=jnp.int32)
    same_before = (
        (destination[None, :] == destination[:, None])
        & row_valid[None, :]
        & (slot_ids[None, :] < slot_ids[:, None])
    )
    rank_in_dest = jnp.sum(same_before.astype(jnp.int32), axis=1)
    capacity = (col_slots + row_count - 1) // row_count
    owner_ids = jnp.arange(owner_count, dtype=jnp.int32)
    capacity_ids = jnp.arange(capacity, dtype=jnp.int32)
    selection = (
        row_valid[None, None, :]
        & (destination[None, None, :] == owner_ids[:, None, None])
        & (rank_in_dest[None, None, :] == capacity_ids[None, :, None])
    )
    flattened = contribution.reshape(row_slots, -1)
    send_buffer = jnp.einsum(
        "oka,ax->okx",
        selection.astype(jnp.float32),
        flattened,
        precision=HIGHEST,
        preferred_element_type=jnp.float32,
    )
    chosen_slot = jnp.sum(jnp.where(selection, parent_row_slot[None, None, :], 0), axis=2)
    send_slots = jnp.where(jnp.any(selection, axis=2), chosen_slot, -1)
    received, received_slots = (
        lax.all_to_all(send_buffer, ("leaf", "row"), split_axis=0, concat_axis=0, tiled=True),
        lax.all_to_all(send_slots, ("leaf", "row"), split_axis=0, concat_axis=0, tiled=True),
    )
    received = received.reshape(leaf_count, row_count, capacity, -1)
    received_slots = received_slots.reshape(leaf_count, row_count, capacity)
    parent_local = parent[:, 0, 0, :, :, 0, :]
    parent_rows = parent_local.shape[0]
    parent_cols = parent_local.shape[2]
    row_place = (
        received_slots[None] == jnp.arange(parent_rows, dtype=jnp.int32)[:, None, None, None]
    ).astype(jnp.float32)
    by_leaf = jnp.einsum(
        "slrk,lrkx->slx", row_place, received, precision=HIGHEST, preferred_element_type=jnp.float32
    )
    by_leaf = by_leaf.reshape(parent_rows, leaf_count, TILE, col_slots, TILE)
    col_match = (col_tiles - pivot_tiles)[:, None] == entry_ids[None, :]
    col_targets = jnp.sum(jnp.where(col_match[None], tile_map[:, None, :], 0), axis=2)
    col_valid = col_tiles >= pivot_tiles
    parent_slot_ids = jnp.arange(parent_cols, dtype=jnp.int32)
    col_place = (
        col_valid[None, None, :]
        & (col_targets[:, None, :] // col_count == parent_slot_ids[None, :, None])
    ).astype(jnp.float32)
    assembled = jnp.einsum(
        "sltbv,lub->stuv", by_leaf, col_place, precision=HIGHEST, preferred_element_type=jnp.float32
    )
    new_parent = (parent_local + assembled).reshape(parent.shape)
    return (factored, new_parent)


def solution(mesh):
    return jax.shard_map(
        per_device,
        mesh=mesh,
        in_specs=(
            P("leaf", None, "row", None, None, "col", None),
            P(None, "leaf", "row", None, None, "col", None),
            P(),
            P(),
        ),
        out_specs=(
            P("leaf", None, "row", None, None, "col", None),
            P(None, "leaf", "row", None, None, "col", None),
        ),
        check_vma=False,
    )
```

profile of v0, /device:TPU:1, one launch (start us, length us, event | category | flops | bytes accessed | tf_op | source)
XLA Modules:
  0.0 995.7 jit_solution(4092188100553603286)
XLA Ops:
  7.2 4.6 copy.98
  13.8 103.2 %all-reduce.14.cloned.1.call-done = (f32[8,128,128]{1,2,0:T(8,128)}, f32[8,128,128]{1,2,0:T(8,128)}, f32[8,128,128]{1,2,0:T(8,128)}, f32[8,128,128]{1,2,0:T(8,128)}) async-done(((f32[8,128,128]{1,2,0:T(8,128)}, f32[8,128,128]{1,2,0:T(8,128)}, f32[8,128,128]{1,2,0:T(8,128)}, f32[8,128,128]{1,2,0:T(8,128)}), (f32[8,128,128]{1,2,0:T(8,128)}, f32[8,128,128]{1,2,0:T(8,128)}, f32[8,128,128]{1,2,0:T(8,128)}, ...) | async-done | bytes 2097168 | tf_op jit(solution)/shard_map/psum | solution.py:17
  124.1 41.6 %all-gather.5.cloned.1.call-done = f32[1,1024,512]{1,2,0:T(8,128)} async-done(((f32[1,128,512]{1,2,0:T(8,128)}), f32[1,1024,512]{1,2,0:T(8,128)}) %all-gather.5.cloned.1.call-update) | async-done | bytes 2097168 | tf_op jit(solution)/shard_map/all_gather | solution.py:78
  165.7 2.3 slice_bitcast_fusion.1
  172.0 11.7 %cholesky.286 = f32[128,128]{1,0:T(8,128)S(1)} custom-call(f32[128,128]{1,0:T(8,128)S(1)} %cholesky.426), custom_call_target="Cholesky" | custom-call | tf_op jit(solution)/shard_map/jit(cholesky)/cholesky | solution.py:80
  183.8 9.8 custom-call.27
  196.2 11.7 %cholesky.305 = f32[128,128]{1,0:T(8,128)S(1)} custom-call(f32[128,128]{1,0:T(8,128)S(1)} %cholesky.430), custom_call_target="Cholesky" | custom-call | tf_op jit(solution)/shard_map/jit(cholesky)/cholesky | solution.py:80
  207.9 10.0 custom-call.28
  219.5 11.7 %cholesky.326 = f32[128,128]{1,0:T(8,128)S(1)} custom-call(f32[128,128]{1,0:T(8,128)S(1)} %cholesky.435), custom_call_target="Cholesky" | custom-call | tf_op jit(solution)/shard_map/jit(cholesky)/cholesky | solution.py:80
  231.2 9.8 custom-call.29
  242.5 11.7 %cholesky.343 = f32[128,128]{1,0:T(8,128)S(1)} custom-call(f32[128,128]{1,0:T(8,128)S(1)} %convolution_subtract_fusion.9), custom_call_target="Cholesky" | custom-call | tf_op jit(solution)/shard_map/jit(cholesky)/cholesky | solution.py:80
  260.8 11.7 %while.10 = (s32[]{:T(128)}, f32[512,512]{1,0:T(8,128)}, s32[4,2]{0,1:T(2,128)S(1)}, f32[4,128,128]{2,1,0:T(8,128)S(1)}, s32[]{:T(128)}) while((s32[]{:T(128)}, f32[512,512]{1,0:T(8,128)}, s32[4,2]{0,1:T(2,128)S(1)}, f32[4,128,128]{2,1,0:T(8,128)S(1)}, s32[]{:T(128)}) %tuple.99), condition=%wide.while_cond.4, body=%wide.while_body.4.sunk | while | flops 2 | bytes 131189 | solution.py:82
  261.4 2.2 bitcast_dynamic-update-slice_fusion.4
  264.4 2.2 bitcast_dynamic-update-slice_fusion.4
  267.3 2.2 bitcast_dynamic-update-slice_fusion.4
  270.3 2.2 bitcast_dynamic-update-slice_fusion.4
  272.5 39.3 %custom-call.30 = f32[4,128,128]{1,2,0:T(8,128)S(1)} custom-call(f32[4,128,128]{2,1,0:T(8,128)S(1)} %get-tuple-element.82), custom_call_target="InvertDiagBlocksLowerTriangular" | custom-call | tf_op jit(solution)/shard_map/triangular_solve/custom-call.3 | solution.py:82
  314.9 2.7 convolution_subtract_fusion.1
  318.3 3.8 fusion.18
  327.4 3.9 pad_maximum_fusion
  331.2 2.9 copy.104
  334.2 2.9 copy.105
  337.1 4.0 select_select_fusion.3
  341.1 2.9 copy.106
  346.0 79.9 %all-reduce.8.cloned.1.call-done = f32[4,2,128,512]{3,2,0,1:T(8,128)} async-done(((f32[4,2,128,512]{3,2,0,1:T(8,128)}), f32[4,2,128,512]{3,2,0,1:T(8,128)}) %all-reduce.8.cloned.1.call-update) | async-done | bytes 2097168 | tf_op jit(solution)/shard_map/psum | solution.py:17
  425.9 5.8 negate_add_fusion.1
  433.2 101.6 %all-reduce.12.cloned.1.call-done = (f32[8,128,128]{1,2,0:T(8,128)}, f32[8,128,128]{1,2,0:T(8,128)}, f32[8,128,128]{1,2,0:T(8,128)}, f32[8,128,128]{1,2,0:T(8,128)}) async-done(((f32[8,128,128]{1,2,0:T(8,128)}, f32[8,128,128]{1,2,0:T(8,128)}, f32[8,128,128]{1,2,0:T(8,128)}, f32[8,128,128]{1,2,0:T(8,128)}), (f32[8,128,128]{1,2,0:T(8,128)}, f32[8,128,128]{1,2,0:T(8,128)}, f32[8,128,128]{1,2,0:T(8,128)}, ...) | async-done | bytes 2097168 | tf_op jit(solution)/shard_map/psum | solution.py:17
  539.3 3.0 copy.112
  542.4 41.1 %all-gather.7.cloned.1.call-done = f32[1,1024,512]{1,2,0:T(8,128)} async-done(((f32[1,128,512]{1,2,0:T(8,128)}), f32[1,1024,512]{1,2,0:T(8,128)}) %all-gather.7.cloned.1.call-update) | async-done | bytes 2097168 | tf_op jit(solution)/shard_map/all_gather | solution.py:78
  583.5 2.3 slice_bitcast_fusion
  589.7 11.7 %cholesky.358 = f32[128,128]{1,0:T(8,128)S(1)} custom-call(f32[128,128]{1,0:T(8,128)S(1)} %cholesky.439), custom_call_target="Cholesky" | custom-call | tf_op jit(solution)/shard_map/jit(cholesky)/cholesky | solution.py:80
  601.6 9.8 custom-call.31
  614.0 11.7 %cholesky.377 = f32[128,128]{1,0:T(8,128)S(1)} custom-call(f32[128,128]{1,0:T(8,128)S(1)} %cholesky.443), custom_call_target="Cholesky" | custom-call | tf_op jit(solution)/shard_map/jit(cholesky)/cholesky | solution.py:80
  625.7 10.0 %custom-call.32 = f32[1,128,128]{1,2,0:T(8,128)S(1)} custom-call(f32[1,128,128]{2,1,0:T(8,128)S(1)} %get-tuple-element.150), custom_call_target="InvertDiagBlocksLowerTriangular" | custom-call | tf_op jit(solution)/shard_map/jit(cholesky)/cholesky | solution.py:80
  637.3 11.7 %cholesky.398 = f32[128,128]{1,0:T(8,128)S(1)} custom-call(f32[128,128]{1,0:T(8,128)S(1)} %cholesky.448), custom_call_target="Cholesky" | custom-call | tf_op jit(solution)/shard_map/jit(cholesky)/cholesky | solution.py:80
  649.0 9.8 custom-call.33
  660.3 11.7 %cholesky.415 = f32[128,128]{1,0:T(8,128)S(1)} custom-call(f32[128,128]{1,0:T(8,128)S(1)} %convolution_subtract_fusion.8), custom_call_target="Cholesky" | custom-call | tf_op jit(solution)/shard_map/jit(cholesky)/cholesky | solution.py:80
  679.1 11.4 %while.11 = (s32[]{:T(128)}, f32[512,512]{1,0:T(8,128)}, s32[4,2]{0,1:T(2,128)S(1)}, f32[4,128,128]{2,1,0:T(8,128)S(1)}, s32[]{:T(128)}) while((s32[]{:T(128)}, f32[512,512]{1,0:T(8,128)}, s32[4,2]{0,1:T(2,128)S(1)}, f32[4,128,128]{2,1,0:T(8,128)S(1)}, s32[]{:T(128)}) %tuple.119), condition=%wide.while_cond.4.clone, body=%wide.while_body.4.clone.sunk | while | flops 2 | bytes 131189 | solution.py:82
  679.7 2.2 bitcast_dynamic-update-slice_fusion.5
  682.6 2.2 bitcast_dynamic-update-slice_fusion.5
  685.4 2.2 bitcast_dynamic-update-slice_fusion.5
  690.5 39.3 %custom-call.34 = f32[4,128,128]{1,2,0:T(8,128)S(1)} custom-call(f32[4,128,128]{2,1,0:T(8,128)S(1)} %get-tuple-element.83), custom_call_target="InvertDiagBlocksLowerTriangular" | custom-call | tf_op jit(solution)/shard_map/triangular_solve/custom-call.3 | solution.py:82
  734.4 2.7 convolution_subtract_fusion
  737.7 3.8 fusion.15
  746.3 3.0 copy.113
  749.3 4.8 pad_maximum_fusion.1
  754.1 2.9 copy.114
  757.0 3.1 copy.115
  760.1 4.0 select_select_fusion
  764.1 2.9 copy.116
  767.9 9.3 all-to-all-start.1
  779.0 2.9 copy.132
  781.9 67.1 %all-reduce.10.cloned.1.call-done = f32[4,2,128,512]{3,2,0,1:T(8,128)} async-done(((f32[4,2,128,512]{3,2,0,1:T(8,128)}), f32[4,2,128,512]{3,2,0,1:T(8,128)}) %all-reduce.10.cloned.1.call-update) | async-done | bytes 2097168 | tf_op jit(solution)/shard_map/psum | solution.py:17
  849.1 5.6 negate_add_fusion
  856.8 3.1 copy.119
  859.9 3.9 reshape.731
  863.8 3.5 convolution_bitcast_fusion
  867.3 6.3 copy.120
  873.6 8.6 all-to-all-start
  882.9 3.6 copy.123
  886.5 88.3 %all-to-all-done = f32[16,1,65536]{2,1,0:T(1,128)} async-done(((f32[16,1,65536]{2,1,0:T(1,128)}), f32[16,1,65536]{2,1,0:T(1,128)}, u32[]{:S(2)}, u32[]{:S(2)}) %all-to-all-start) | async-done | bytes 4194336 | tf_op jit(solution)/shard_map/all_to_all | solution.py:149
  974.8 7.8 convolution_bitcast_fusion.1
  982.6 3.1 reshape.733
  985.8 2.8 fusion.14
  (171 shorter events, 75.7 us)
Async XLA Ops:
  7.2 109.8 %all-reduce.14.cloned.1.call-start = ((), (), s32[]{:S(2)}) async-start(), calls=%async_computation.7 | async-start | bytes 4194304 | tf_op jit(solution)/shard_map/psum | solution.py:17
  11.8 2.0 copy-start
  13.8 151.9 %all-gather.5.cloned.1.call-start = ((), (), s32[]{:S(2)}) async-start(), calls=%async_computation.4 | async-start | bytes 2359296 | tf_op jit(solution)/shard_map/all_gather | solution.py:78
  117.0 2.3 copy-start.14
  117.0 2.3 copy-start.12
  118.1 3.4 copy-start.16
  119.3 1.3 copy-start.5
  121.4 304.5 %all-reduce.8.cloned.1.call-start = ((), (), s32[]{:S(2)}) async-start(), calls=%async_computation.2 | async-start | bytes 4194304 | tf_op jit(solution)/shard_map/psum | solution.py:17
  171.0 1.0 copy-start.7
  318.3 3.8 copy-start.4
  334.2 2.9 copy-start.11
  344.1 190.7 %all-reduce.12.cloned.1.call-start = ((), (), s32[]{:S(2)}) async-start(), calls=%async_computation.6 | async-start | bytes 4194304 | tf_op jit(solution)/shard_map/psum | solution.py:17
  433.1 150.4 %all-gather.7.cloned.1.call-start = ((), (), s32[]{:S(2)}) async-start(), calls=%async_computation.5 | async-start | bytes 2359296 | tf_op jit(solution)/shard_map/all_gather | solution.py:78
  534.8 2.3 copy-start.15
  534.8 2.3 copy-start.13
  537.1 1.3 copy-start.6
  539.2 309.9 %all-reduce.10.cloned.1.call-start = ((), (), s32[]{:S(2)}) async-start(), calls=%async_computation.3 | async-start | bytes 4194304 | tf_op jit(solution)/shard_map/psum | solution.py:17
  588.8 1.0 copy-start.8
  729.8 4.6 copy-start.1
  737.7 3.8 copy-start.3
  757.0 3.1 copy-start.10
  767.9 105.7 %all-to-all-start.1 = ((s32[16,1,1]{2,1,0:T(1,128)}), s32[16,1,1]{2,1,0:T(1,128)S(1)}, u32[]{:S(2)}, u32[]{:S(2)}) async-start(s32[16,1,1]{2,1,0:T(1,128)} %copy.121), calls=%async_computation.1 | async-start | bytes 16384 | tf_op jit(solution)/shard_map/all_to_all | solution.py:150
  849.1 5.7 copy-start.2
  873.6 101.2 %all-to-all-start = ((f32[16,1,65536]{2,1,0:T(1,128)}), f32[16,1,65536]{2,1,0:T(1,128)}, u32[]{:S(2)}, u32[]{:S(2)}) async-start(f32[16,1,65536]{2,1,0:T(1,128)} %copy.120), calls=%async_computation | async-start | bytes 8388608 | tf_op jit(solution)/shard_map/all_to_all | solution.py:149
  982.6 3.1 copy-start.9
Sparse Core Ops, SparseCore 0:
  13.5 103.4 all-reduce.13
  121.5 44.1 all-gather.4
  344.2 81.6 all-reduce.7
  433.2 101.4 all-reduce.11
  539.3 44.1 all-gather.6
  767.2 81.8 all-reduce.9
where the time goes:
time: 1010 us; the launch traced here: 996 us
  waiting for transfers between devices  523 us (52%)
  other arithmetic  267 us (26%)
  local copies, waits for them, and re-layouts  105 us (10%)
  matrix products  61.2 us (6%)
  between operations  21 us (2%)
  starting transfers between devices  18.2 us (2%)
    psum x4, waiting for transfers between devices, spread(): return lax.psum(kept, axis)  352 us
    another operation x29, other arithmetic, per_device(): lower_factor = jnp.linalg.cholesky(diagonal_block)  158 us
    another operation x7, other arithmetic, per_device(): lax.linalg.triangular_solve(lower_factor, factor_flattened, left_side=Fal...  90.5 us
    all_to_all x1, waiting for transfers between devices, per_device(): lax.all_to_all(send_buffer, ('leaf', 'row'), split_axis=0, concat_axis=0,...  88.3 us
    all_gather x2, waiting for transfers between devices, per_device(): lax.all_gather(panel_block[factor_slot_index], 'row', axis=0, tiled=True)  82.7 us
    another operation x29, local copies, waits for them, and re-layouts, per_device(): lax.linalg.triangular_solve(lower_factor, factor_flattened, left_side=Fal...  28.8 us
    another operation x14, matrix products, per_device(): lax.linalg.triangular_solve(lower_factor, factor_flattened, left_side=Fal...  24.7 us
  transfers between devices with their start and end apart: 8, of which 7 were waited for; matrix products, arithmetic and copies ran while one was open for 4% of the time, Pallas kernels for 0%

commit v1 on v0

--- a/solution.py
+++ b/solution.py
@@ -38,77 +38,51 @@
     local_front = front[0, :, 0, :, :, 0, :]
     row_slots = local_front.shape[0]
     col_slots = local_front.shape[2]
-    panel_tiles = PB // TILE
     pivot_tiles = NPIV // TILE
+    assert pivot_tiles == row_count and pivot_tiles <= col_count
     row_tiles = jnp.arange(row_slots, dtype=jnp.int32) * row_count + row_index
     col_tiles = jnp.arange(col_slots, dtype=jnp.int32) * col_count + col_index
 
-    def fetch_panel(working, panel_index):
-        pieces = []
-        for offset in range(panel_tiles):
-            column = panel_index * panel_tiles + offset
-            column_tile = working[:, :, column // col_count, :]
-            pieces.append(spread(column_tile, "col", column % col_count))
-        return jnp.concatenate(pieces, axis=2)
-
-    def write_factor(working, factor, panel_index):
-        first_column = panel_index * panel_tiles
-        slot_values = sorted(
-            set([(first_column + offset) // col_count for offset in range(panel_tiles)])
-        )
-        for slot_index in slot_values:
-            current = working[:, :, slot_index, :]
-            for offset in range(panel_tiles):
-                column = first_column + offset
-                if column // col_count == slot_index:
-                    current = jnp.where(
-                        col_index == column % col_count,
-                        factor[:, :, offset * TILE : (offset + 1) * TILE],
-                        current,
-                    )
-            working = working.at[:, :, slot_index, :].set(current)
-        return working
-
     working = local_front
-    panel_block = fetch_panel(working, 0)
-    for panel_index in range(PANELS):
-        first_tile = panel_index * panel_tiles
-        factor_slot_index = first_tile // row_count
-        start_row = first_tile % row_count
-        gathered = lax.all_gather(panel_block[factor_slot_index], "row", axis=0, tiled=True)
-        diagonal_block = gathered[start_row * TILE : (start_row + panel_tiles) * TILE]
-        lower_factor = jnp.linalg.cholesky(diagonal_block)
-        factor_flattened = panel_block.reshape(row_slots * TILE, PB)
-        solved = lax.linalg.triangular_solve(
-            lower_factor, factor_flattened, left_side=False, lower=True, transpose_a=True
-        )
-        solved = solved.reshape(row_slots, TILE, PB)
-        offset_tile = jnp.clip(row_index - start_row, 0, panel_tiles - 1)
-        diagonal_rows = lax.dynamic_slice_in_dim(lower_factor, offset_tile * TILE, TILE, 0)
-        in_panel = (row_tiles >= first_tile) & (row_tiles < first_tile + panel_tiles)
-        factor_factor = jnp.where(in_panel[:, None, None], diagonal_rows[None], solved)
-        factor_factor = jnp.where((row_tiles >= first_tile)[:, None, None], factor_factor, 0.0)
-        next_rows = jnp.where(
-            (row_tiles >= first_tile + panel_tiles)[:, None, None], factor_factor, 0.0
-        )
-        group_size = col_count // row_count
-        owner_rows = spread(next_rows, "row", col_index % row_count)
-        grouped = owner_rows.reshape(col_slots, group_size, TILE, PB)
-        column_factor = lax.dynamic_index_in_dim(grouped, col_index // row_count, 1, keepdims=False)
-        column_factor = jnp.where(
-            (col_tiles >= first_tile + panel_tiles)[:, None, None], column_factor, 0.0
-        )
-        factor, next_rows, column_factor = (factor_factor, next_rows, column_factor)
-        working = update_slots(working, next_rows, column_factor, 0, col_slots)
-        upcoming = (
-            fetch_panel(working, panel_index + 1) if panel_index + 1 < PANELS else panel_block
-        )
-        working = write_factor(working, factor, panel_index)
-        panel_block = upcoming
-    upper_part = (row_tiles < pivot_tiles)[:, None, None, None] & (col_tiles >= pivot_tiles)[
-        None, None, :, None
-    ]
-    working = jnp.where(upper_part, 0.0, working)
+    top_rows = lax.all_gather(working[0], "row", axis=0, tiled=False)
+    column_panel = top_rows.transpose(2, 3, 0, 1).reshape(col_slots, TILE, NPIV)
+    first_cols = lax.all_gather(working[:, :, 0, :], "col", axis=0, tiled=False)
+    row_panel = first_cols[:pivot_tiles].transpose(1, 2, 0, 3).reshape(row_slots, TILE, NPIV)
+    diagonal_block = lax.all_gather(row_panel[0], "row", axis=0, tiled=True)
+    lower_factor = jnp.linalg.cholesky(diagonal_block)
+    stacked = jnp.concatenate(
+        [row_panel[1:].reshape(-1, NPIV), column_panel.reshape(-1, NPIV)], axis=0
+    )
+    solved = lax.linalg.triangular_solve(
+        lower_factor, stacked, left_side=False, lower=True, transpose_a=True
+    )
+    trailing_rows = (row_slots - 1) * TILE
+    row_factor = solved[:trailing_rows].reshape(row_slots - 1, TILE, NPIV)
+    column_factor = solved[trailing_rows:].reshape(col_slots, TILE, NPIV)
+    column_factor = jnp.where(
+        (col_tiles >= pivot_tiles)[:, None, None], column_factor, 0.0
+    )
+    product = jnp.einsum(
+        "atk,bsk->atbs",
+        row_factor,
+        column_factor,
+        precision=HIGHEST,
+        preferred_element_type=jnp.float32,
+    )
+    trailing = working[1:] - product
+    own_col = jnp.minimum(col_index, pivot_tiles - 1)
+    row_factor_cols = lax.dynamic_slice_in_dim(row_factor, own_col * TILE, TILE, 2)
+    is_factor_col = (col_tiles < pivot_tiles)[None, None, :, None]
+    trailing = jnp.where(is_factor_col, row_factor_cols[:, :, None, :], trailing)
+    diag_rows = lax.dynamic_slice_in_dim(lower_factor, row_index * TILE, TILE, 0)
+    diag_tile = lax.dynamic_slice_in_dim(diag_rows, own_col * TILE, TILE, 1)
+    local_ids = jnp.arange(TILE, dtype=jnp.int32)
+    global_row = row_index * TILE + local_ids[:, None]
+    global_col = own_col * TILE + local_ids[None, :]
+    diag_tile = jnp.where(global_row >= global_col, diag_tile, 0.0)
+    top = jnp.where(is_factor_col[0], diag_tile[:, None, :], 0.0)
+    top = jnp.broadcast_to(top, working[0].shape)
+    working = jnp.concatenate([top[None], trailing], axis=0)
     factored = working.reshape(front.shape)
     contribution = jnp.where((col_tiles >= pivot_tiles)[None, None, :, None], working, 0.0)
     contrib_count = tile_map.shape[1]

time: 1010 us -> 737 us (0.73)
  waiting for transfers between devices: 523 us -> 245 us
  matrix products: 61.2 us -> 98.3 us
  local copies, waits for them, and re-layouts: 105 us -> 84.2 us
    psum x4 -> x0, waiting for transfers between devices: 352 us -> none  [spread(): return lax.psum(kept, axis)]
    all_gather x2 -> x3, waiting for transfers between devices: 82.7 us -> 157 us  [the longest x1 78.9 us: per_device(): first_cols = lax.all_gather(working[:, :, 0, :], 'col', axis=0, tiled=False)]
    another operation x14 -> x15, matrix products: 24.7 us -> 51.9 us  [per_device(): lax.linalg.triangular_solve(lower_factor, stacked, left_side=False, lower...]
    reshape x5 -> x0, local copies, waits for them, and re-layouts: 15.7 us -> none  [the longest x2 5.99 us: per_device(): solved = solved.reshape(row_slots, TILE, PB)]
    another operation x29 -> x30, other arithmetic: 158 us -> 172 us  [per_device(): lower_factor = jnp.linalg.cholesky(diagonal_block)]
    another operation x12 -> x14, matrix products: 10.9 us -> 23.1 us  [per_device(): lower_factor = jnp.linalg.cholesky(diagonal_block)]
    select_n x5 -> x4, other arithmetic: 12.6 us -> 1.51 us  [the longest x1 1.01 us: per_device(): diag_tile = jnp.where(global_row >= global_col, diag_tile, 0.0)]
    another operation x29 -> x25, local copies, waits for them, and re-layouts: 28.8 us -> 23.1 us  [per_device(): lax.linalg.triangular_solve(lower_factor, factor_flattened, left_side=Fal...]
  transfers between devices with their start and end apart: 8 -> 5, of which waited for: 7 -> 4; matrix products, arithmetic and copies ran while one was open for 4% -> 58% of each run, Pallas kernels for 0% -> 0%
where the time goes in v1:
time: 737 us; the launch traced here: 731 us
  other arithmetic  266 us (36%)
  waiting for transfers between devices  245 us (33%)
  matrix products  98.3 us (13%)
  local copies, waits for them, and re-layouts  84.2 us (11%)
  between operations  19.4 us (3%)
  starting transfers between devices  18 us (2%)
    another operation x30, other arithmetic, per_device(): lower_factor = jnp.linalg.cholesky(diagonal_block)  172 us
    all_to_all x1, waiting for transfers between devices, per_device(): lax.all_to_all(send_buffer, ('leaf', 'row'), split_axis=0, concat_axis=0,...  88.3 us
    another operation x3, other arithmetic, per_device(): lax.linalg.triangular_solve(lower_factor, stacked, left_side=False, lower...  85.7 us
    all_gather x1, waiting for transfers between devices, per_device(): first_cols = lax.all_gather(working[:, :, 0, :], 'col', axis=0, tiled=False)  78.9 us
    all_gather x1, waiting for transfers between devices, per_device(): diagonal_block = lax.all_gather(row_panel[0], 'row', axis=0, tiled=True)  55.7 us
    another operation x15, matrix products, per_device(): lax.linalg.triangular_solve(lower_factor, stacked, left_side=False, lower...  51.9 us
    another operation x24, local copies, waits for them, and re-layouts  23.1 us
    another operation x14, matrix products, per_device(): lower_factor = jnp.linalg.cholesky(diagonal_block)  23.1 us
  transfers between devices with their start and end apart: 5, of which 4 were waited for; matrix products, arithmetic and copies ran while one was open for 58% of the time, Pallas kernels for 0%

profile of v1, /device:TPU:1, one launch (start us, length us, event | category | flops | bytes accessed | tf_op | source)
XLA Modules:
  0.0 730.9 jit_solution(1884247141406783807)
XLA Ops:
  12.2 78.9 %all-gather.8.cloned.1.call-done = f32[128,128,1,128]{3,1,2,0:T(8,128)} async-done(((f32[8,128,1,128]{3,1,2,0:T(8,128)}), f32[128,128,1,128]{3,1,2,0:T(8,128)}) %all-gather.8.cloned.1.call-update) | async-done | bytes 8388624 | tf_op jit(solution)/shard_map/all_gather | solution.py:49
  91.0 2.2 slice-done
  93.2 2.4 copy.88
  99.9 7.7 %all-to-all-start.1 = ((s32[16,1,1]{2,1,0:T(1,128)}), s32[16,1,1]{2,1,0:T(1,128)S(1)}, u32[]{:S(2)}, u32[]{:S(2)}) async-start(s32[16,1,1]{2,1,0:T(1,128)} %copy.67), calls=%async_computation.1 | async-start | bytes 16384 | tf_op jit(solution)/shard_map/all_to_all | solution.py:124
  107.8 22.4 %all-gather.10.cloned.1.call-done = f32[8,1,1,128,4,1,128]{6,3,5,4,2,1,0:T(8,128)} async-done(((f32[1,1,1,128,4,1,128]{6,3,5,4,2,1,0:T(8,128)}), f32[8,1,1,128,4,1,128]{6,3,5,4,2,1,0:T(8,128)}) %all-gather.10.cloned.1.call-update) | async-done | bytes 2097168 | tf_op jit(solution)/shard_map/all_gather | solution.py:47
  132.2 2.3 slice.280
  134.5 2.7 bitcast_dynamic-update-slice_fusion.1
  139.0 55.7 %all-gather.6.cloned.1.call-done = f32[1024,1024]{0,1:T(8,128)} async-done(((f32[128,1024]{0,1:T(8,128)}), f32[1024,1024]{0,1:T(8,128)}) %all-gather.6.cloned.1.call-update) | async-done | bytes 4194320 | tf_op jit(solution)/shard_map/all_gather | solution.py:51
  194.6 5.5 copy.59
  200.2 4.4 fusion.2
  206.6 11.7 %cholesky.223 = f32[128,128]{1,0:T(8,128)S(1)} custom-call(f32[128,128]{1,0:T(8,128)S(1)} %cholesky.580), custom_call_target="Cholesky" | custom-call | tf_op jit(solution)/shard_map/jit(cholesky)/cholesky | solution.py:52
  218.4 9.8 %custom-call.62 = f32[1,128,128]{1,2,0:T(8,128)S(1)} custom-call(f32[1,128,128]{2,1,0:T(8,128)S(1)} %get-tuple-element.80), custom_call_target="InvertDiagBlocksLowerTriangular" | custom-call | tf_op jit(solution)/shard_map/jit(cholesky)/cholesky | solution.py:52
  228.2 2.5 cholesky.255
  230.7 2.4 constant_dynamic-update-slice_fusion.30
  234.6 11.9 %cholesky.244 = f32[128,128]{1,0:T(8,128)S(1)} custom-call(f32[128,128]{1,0:T(8,128)S(1)} %cholesky.584), custom_call_target="Cholesky" | custom-call | tf_op jit(solution)/shard_map/jit(cholesky)/cholesky | solution.py:52
  247.2 9.8 %custom-call.63 = f32[1,128,128]{1,2,0:T(8,128)S(1)} custom-call(f32[1,128,128]{2,1,0:T(8,128)S(1)} %get-tuple-element.77), custom_call_target="InvertDiagBlocksLowerTriangular" | custom-call | tf_op jit(solution)/shard_map/jit(cholesky)/cholesky | solution.py:52
  258.2 2.1 convolution_subtract_fusion.7
  260.3 11.7 %cholesky.468 = f32[128,128]{1,0:T(8,128)S(1)} custom-call(f32[128,128]{1,0:T(8,128)S(1)} %cholesky.589), custom_call_target="Cholesky" | custom-call | tf_op jit(solution)/shard_map/jit(cholesky)/cholesky | solution.py:52
  273.3 9.8 %custom-call.64 = f32[1,128,128]{1,2,0:T(8,128)S(1)} custom-call(f32[1,128,128]{2,1,0:T(8,128)S(1)} %get-tuple-element.74), custom_call_target="InvertDiagBlocksLowerTriangular" | custom-call | tf_op jit(solution)/shard_map/jit(cholesky)/cholesky | solution.py:52
  284.3 2.3 convolution_subtract_fusion.8
  286.7 12.1 %cholesky.487 = f32[128,128]{1,0:T(8,128)S(1)} custom-call(f32[128,128]{1,0:T(8,128)S(1)} %cholesky.594), custom_call_target="Cholesky" | custom-call | tf_op jit(solution)/shard_map/jit(cholesky)/cholesky | solution.py:52
  300.0 9.8 %custom-call.65 = f32[1,128,128]{1,2,0:T(8,128)S(1)} custom-call(f32[1,128,128]{2,1,0:T(8,128)S(1)} %get-tuple-element.71), custom_call_target="InvertDiagBlocksLowerTriangular" | custom-call | tf_op jit(solution)/shard_map/jit(cholesky)/cholesky | solution.py:52
  310.9 2.3 convolution_subtract_fusion.9
  313.3 11.7 %cholesky.506 = f32[128,128]{1,0:T(8,128)S(1)} custom-call(f32[128,128]{1,0:T(8,128)S(1)} %cholesky.599), custom_call_target="Cholesky" | custom-call | tf_op jit(solution)/shard_map/jit(cholesky)/cholesky | solution.py:52
  326.4 9.9 %custom-call.66 = f32[1,128,128]{1,2,0:T(8,128)S(1)} custom-call(f32[1,128,128]{2,1,0:T(8,128)S(1)} %get-tuple-element.68), custom_call_target="InvertDiagBlocksLowerTriangular" | custom-call | tf_op jit(solution)/shard_map/jit(cholesky)/cholesky | solution.py:52
  337.3 2.3 convolution_subtract_fusion.10
  339.6 11.7 %cholesky.526 = f32[128,128]{1,0:T(8,128)S(1)} custom-call(f32[128,128]{1,0:T(8,128)S(1)} %cholesky.604), custom_call_target="Cholesky" | custom-call | tf_op jit(solution)/shard_map/jit(cholesky)/cholesky | solution.py:52
  352.6 9.8 %custom-call.67 = f32[1,128,128]{1,2,0:T(8,128)S(1)} custom-call(f32[1,128,128]{2,1,0:T(8,128)S(1)} %get-tuple-element.65), custom_call_target="InvertDiagBlocksLowerTriangular" | custom-call | tf_op jit(solution)/shard_map/jit(cholesky)/cholesky | solution.py:52
  363.3 2.0 convolution_subtract_fusion.11
  365.4 11.9 %cholesky.546 = f32[128,128]{1,0:T(8,128)S(1)} custom-call(f32[128,128]{1,0:T(8,128)S(1)} %cholesky.609), custom_call_target="Cholesky" | custom-call | tf_op jit(solution)/shard_map/jit(cholesky)/cholesky | solution.py:52
  378.7 9.8 %custom-call.68 = f32[1,128,128]{1,2,0:T(8,128)S(1)} custom-call(f32[1,128,128]{2,1,0:T(8,128)S(1)} %get-tuple-element.62), custom_call_target="InvertDiagBlocksLowerTriangular" | custom-call | tf_op jit(solution)/shard_map/jit(cholesky)/cholesky | solution.py:52
  391.1 11.7 %cholesky.564 = f32[128,128]{1,0:T(8,128)S(1)} custom-call(f32[128,128]{1,0:T(8,128)S(1)} %convolution_subtract_fusion.12), custom_call_target="Cholesky" | custom-call | tf_op jit(solution)/shard_map/jit(cholesky)/cholesky | solution.py:52
  409.7 6.7 fusion.3
  416.4 23.3 %while.1 = (s32[]{:T(128)}, f32[1024,1024]{1,0:T(8,128)}, s32[8,2]{0,1:T(2,128)S(1)}, f32[8,128,128]{2,1,0:T(8,128)S(1)}, s32[]{:T(128)}) while((s32[]{:T(128)}, f32[1024,1024]{1,0:T(8,128)}, s32[8,2]{0,1:T(2,128)S(1)}, f32[8,128,128]{2,1,0:T(8,128)S(1)}, s32[]{:T(128)}) %tuple.72), condition=%wide.while_cond, body=%wide.while_body.sunk | while | flops 2 | bytes 131189 | solution.py:56
  417.0 2.3 bitcast_dynamic-update-slice_fusion.4
  420.0 2.3 bitcast_dynamic-update-slice_fusion.4
  422.9 2.3 bitcast_dynamic-update-slice_fusion.4
  425.8 2.3 bitcast_dynamic-update-slice_fusion.4
  428.7 2.3 bitcast_dynamic-update-slice_fusion.4
  431.6 2.3 bitcast_dynamic-update-slice_fusion.4
  434.5 2.3 bitcast_dynamic-update-slice_fusion.4
  437.5 2.2 bitcast_dynamic-update-slice_fusion.4
  439.7 79.0 %custom-call.69 = f32[8,128,128]{1,2,0:T(8,128)S(1)} custom-call(f32[8,128,128]{2,1,0:T(8,128)S(1)} %get-tuple-element.9), custom_call_target="InvertDiagBlocksLowerTriangular" | custom-call | tf_op jit(solution)/shard_map/triangular_solve | solution.py:56
  518.7 2.1 constant_dynamic-update-slice_fusion.17
  520.8 2.5 convolution_subtract_fusion.3
  524.2 3.7 convolution_subtract_fusion.5
  528.9 4.9 convolution_subtract_fusion.2
  534.9 6.2 fusion.12
  542.0 7.3 %convolution_subtract_fusion.1 = f32[1408,128]{1,0:T(8,128)S(1)} fusion(f32[1408,640]{0,1:T(8,128)S(1)} %get-tuple-element.42, f32[1408,1024]{1,0:T(8,128)} %bitcast_dynamic-update-slice_fusion.2, f32[1024,1024]{1,0:T(8,128)} %get-tuple-element.146), kind=kOutput, calls=%fused_computation.23 | convolution fusion | flops 1384300544 | bytes 5373952 | tf_op jit(solution)/shard_map/triangular_solve | solution.py:56
  550.2 8.6 %convolution_subtract_fusion = f32[1408,128]{1,0:T(8,128)S(1)} fusion(f32[1408,768]{0,1:T(8,128)S(1)} %get-tuple-element.38, f32[1408,1024]{1,0:T(8,128)} %bitcast_dynamic-update-slice_fusion.2, f32[1024,1024]{1,0:T(8,128)} %get-tuple-element.146), kind=kOutput, calls=%fused_computation.22 | convolution fusion | flops 1661124608 | bytes 6160384 | tf_op jit(solution)/shard_map/triangular_solve | solution.py:56
  559.7 10.1 %convolution_subtract_fusion.4 = f32[1408,128]{1,0:T(8,128)S(1)} fusion(f32[1408,896]{0,1:T(8,128)S(1)} %get-tuple-element.34, f32[1408,1024]{1,0:T(8,128)} %bitcast_dynamic-update-slice_fusion.2, f32[1024,1024]{1,0:T(8,128)} %get-tuple-element.146), kind=kOutput, calls=%fused_computation.26 | convolution fusion | flops 1937948672 | bytes 6946816 | tf_op jit(solution)/shard_map/triangular_solve | solution.py:56
  570.7 2.1 slice.281
  573.1 5.1 copy.62
  582.2 9.0 %fusion.23 = f32[7,128,4,128]{3,1,2,0:T(8,128)S(1)} fusion(f32[1,8,1,128,4,1,128]{6,3,4,1,5,2,0:T(8,128)} %copy-done.2, f32[7,128,1024,1]{2,1,3,0:T(8,128)} %bitcast.180, f32[4,128,1024,1]{2,1,0,3:T(8,128)} %bitcast.183, f32[7,128,128]{2,1,0:T(8,128)S(1)} %constant_dynamic-slice_fusion.2, pred[4]{0:T(512)(128)(4,1)S(1)} %get-tuple-element.92), kind=kOutput, calls=%fused_computation.42 | convolution fusion | flops 5638062080 | bytes 9895940 | tf_op jit(solution)/shard_map/atk,bsk->atbs/dot_general | solution.py:65
  591.2 2.4 copy.65
  593.6 3.7 concatenate.33
  597.4 3.8 convolution_bitcast_fusion
  601.2 6.3 copy.66
  607.5 10.2 %all-to-all-start = ((f32[16,1,65536]{2,1,0:T(1,128)}), f32[16,1,65536]{2,1,0:T(1,128)}, u32[]{:S(2)}, u32[]{:S(2)}) async-start(f32[16,1,65536]{2,1,0:T(1,128)} %copy.66), calls=%async_computation | async-start | bytes 8388608 | tf_op jit(solution)/shard_map/all_to_all | solution.py:123
  618.7 3.5 copy.69
  622.2 88.3 %all-to-all-done = f32[16,1,65536]{2,1,0:T(1,128)} async-done(((f32[16,1,65536]{2,1,0:T(1,128)}), f32[16,1,65536]{2,1,0:T(1,128)}, u32[]{:S(2)}, u32[]{:S(2)}) %all-to-all-start) | async-done | bytes 4194336 | tf_op jit(solution)/shard_map/all_to_all | solution.py:123
  710.5 7.8 %convolution_bitcast_fusion.1 = f32[4,2,65536]{2,0,1:T(4,128)} fusion(f32[16,1,65536]{2,1,0:T(1,128)} %all-to-all-done, s32[2,8]{1,0:T(2,128)S(1)} %eq.135), kind=kOutput, calls=%fused_computation.3 | convolution fusion | flops 50331712 | bytes 6291520 | tf_op jit(solution)/shard_map/slrk,lrkx->slx/dot_general | solution.py:134
  718.3 3.0 reshape.514
  721.4 2.8 fusion.27
  (111 shorter events, 50.9 us)
Async XLA Ops:
  7.2 4.2 slice-start.1
  7.2 83.8 %all-gather.8.cloned.1.call-start = ((), (), s32[]{:S(2)}) async-start(), calls=%async_computation.3 | async-start | bytes 8912896 | tf_op jit(solution)/shard_map/all_gather | solution.py:49
  9.1 1.3 copy-start.2
  11.3 118.9 %all-gather.10.cloned.1.call-start = ((), (), s32[]{:S(2)}) async-start(), calls=%async_computation.4 | async-start | bytes 2359296 | tf_op jit(solution)/shard_map/all_gather | solution.py:47
  12.1 182.5 %all-gather.6.cloned.1.call-start = ((), (), s32[]{:S(2)}) async-start(), calls=%async_computation.2 | async-start | bytes 4718592 | tf_op jit(solution)/shard_map/all_gather | solution.py:51
  91.0 2.2 slice-start
  93.2 5.4 copy-start.4
  95.6 1.9 copy-start
  99.9 507.6 %all-to-all-start.1 = ((s32[16,1,1]{2,1,0:T(1,128)}), s32[16,1,1]{2,1,0:T(1,128)S(1)}, u32[]{:S(2)}, u32[]{:S(2)}) async-start(s32[16,1,1]{2,1,0:T(1,128)} %copy.67), calls=%async_computation.1 | async-start | bytes 16384 | tf_op jit(solution)/shard_map/all_to_all | solution.py:124
  204.6 2.0 copy-start.1
  607.5 103.0 %all-to-all-start = ((f32[16,1,65536]{2,1,0:T(1,128)}), f32[16,1,65536]{2,1,0:T(1,128)}, u32[]{:S(2)}, u32[]{:S(2)}) async-start(f32[16,1,65536]{2,1,0:T(1,128)} %copy.66), calls=%async_computation | async-start | bytes 8388608 | tf_op jit(solution)/shard_map/all_to_all | solution.py:123
  622.2 99.2 %copy-start.3 = (f32[4,1,1,128,4,1,128]{6,5,4,3,2,1,0:T(1,128)S(1)}, f32[4,1,1,128,4,1,128]{6,5,4,3,2,1,0:T(1,128)}, u32[]{:S(2)}) copy-start(f32[4,1,1,128,4,1,128]{6,5,4,3,2,1,0:T(1,128)} %param.5) | copy-start | bytes 3145732
Sparse Core Ops, SparseCore 0:
  11.4 79.5 all-gather.7
  92.8 37.3 all-gather.9
  132.5 62.1 all-gather.5

commit v2 on v1

--- a/solution.py
+++ b/solution.py
@@ -28,6 +28,35 @@
     return working.at[:, :, slot_low:slot_high, :].add(-product)
 
 
+def tall_cholesky(diagonal_block, below_rows):
+    size = diagonal_block.shape[0]
+    remaining = jnp.concatenate([diagonal_block, below_rows], axis=0)
+    eye = jnp.eye(TILE, dtype=jnp.float32)
+    diag_columns = []
+    below_columns = []
+    for step in range(size // TILE):
+        low = step * TILE
+        left = size - low - TILE
+        pivot = remaining[:TILE, :TILE]
+        pivot_factor = jnp.linalg.cholesky(pivot)
+        pivot_inverse = lax.linalg.triangular_solve(
+            pivot_factor, eye, left_side=True, lower=True
+        )
+        under = remaining[TILE:, :TILE]
+        solved = jnp.dot(
+            under, pivot_inverse.T, precision=HIGHEST, preferred_element_type=jnp.float32
+        )
+        diag_columns.append(jnp.concatenate([jnp.zeros((low, TILE), jnp.float32), pivot_factor, solved[:left]], axis=0))
+        below_columns.append(solved[left:])
+        if left:
+            update = jnp.dot(
+                solved, solved[:left].T, precision=HIGHEST, preferred_element_type=jnp.float32
+            )
+            remaining = remaining[TILE:, TILE:] - update
+    lower_factor = jnp.concatenate(diag_columns, axis=1)
+    return lower_factor, jnp.concatenate(below_columns, axis=1)
+
+
 def per_device(front, parent, tile_map, col_shift):
     leaf_count = lax.axis_size("leaf")
     row_count = lax.axis_size("row")
@@ -44,18 +73,20 @@
     col_tiles = jnp.arange(col_slots, dtype=jnp.int32) * col_count + col_index
 
     working = local_front
-    top_rows = lax.all_gather(working[0], "row", axis=0, tiled=False)
+    first_tiles = lax.all_gather(working[0, :, 0, :], "col", axis=0, tiled=False)
+    diag_row = first_tiles[:pivot_tiles].transpose(1, 0, 2).reshape(TILE, NPIV)
+    diagonal_block = lax.all_gather(diag_row, "row", axis=0, tiled=True)
+    rest_cols, top_input, diagonal_block = lax.optimization_barrier(
+        (working[1:, :, 0, :], working[0], diagonal_block)
+    )
+    first_cols = lax.all_gather(rest_cols, "col", axis=0, tiled=False)
+    row_panel = first_cols[:pivot_tiles].transpose(1, 2, 0, 3).reshape(row_slots - 1, TILE, NPIV)
+    top_rows = lax.all_gather(top_input, "row", axis=0, tiled=False)
     column_panel = top_rows.transpose(2, 3, 0, 1).reshape(col_slots, TILE, NPIV)
-    first_cols = lax.all_gather(working[:, :, 0, :], "col", axis=0, tiled=False)
-    row_panel = first_cols[:pivot_tiles].transpose(1, 2, 0, 3).reshape(row_slots, TILE, NPIV)
-    diagonal_block = lax.all_gather(row_panel[0], "row", axis=0, tiled=True)
-    lower_factor = jnp.linalg.cholesky(diagonal_block)
     stacked = jnp.concatenate(
-        [row_panel[1:].reshape(-1, NPIV), column_panel.reshape(-1, NPIV)], axis=0
+        [row_panel.reshape(-1, NPIV), column_panel.reshape(-1, NPIV)], axis=0
     )
-    solved = lax.linalg.triangular_solve(
-        lower_factor, stacked, left_side=False, lower=True, transpose_a=True
-    )
+    lower_factor, solved = tall_cholesky(diagonal_block, stacked)
     trailing_rows = (row_slots - 1) * TILE
     row_factor = solved[:trailing_rows].reshape(row_slots - 1, TILE, NPIV)
     column_factor = solved[trailing_rows:].reshape(col_slots, TILE, NPIV)

time: 737 us -> 692 us (0.939)
  other arithmetic: 266 us -> 213 us
  waiting for transfers between devices: 245 us -> 274 us
  matrix products: 98.3 us -> 85.8 us
    another operation x29 -> x8, matrix products: 75 us -> 4.79 us  [tall_cholesky(): lax.linalg.triangular_solve(pivot_factor, eye, left_side=True, lower=True)]
    dot_general x0 -> x15, matrix products: none -> 60.6 us  [the longest x7 38 us: tall_cholesky(): jnp.dot(solved, solved[:left].T, precision=HIGHEST, preferred_element_typ...]
    another operation x33 -> x40, other arithmetic: 258 us -> 199 us  [the longest x24 105 us: tall_cholesky(): pivot_factor = jnp.linalg.cholesky(pivot)]
    all_gather x3 -> x4, waiting for transfers between devices: 157 us -> 184 us  [the longest x1 73.8 us: per_device(): first_cols = lax.all_gather(rest_cols, 'col', axis=0, tiled=False)]
    another operation x33 -> x2, local copies, waits for them, and re-layouts: 25.6 us -> 5.17 us  [the longest x1 5.16 us: per_device(): row_panel.reshape(-1, NPIV)]
    unnamed x14 -> x97, local copies, waits for them, and re-layouts: 14 us -> 33.1 us
  transfers between devices with their start and end apart: 5 -> 6, of which waited for: 4 -> 5; matrix products, arithmetic and copies ran while one was open for 58% -> 50% of each run, Pallas kernels for 0% -> 0%
where the time goes in v2:
time: 692 us; the launch traced here: 682 us
  waiting for transfers between devices  274 us (40%)
  other arithmetic  213 us (31%)
  matrix products  85.8 us (12%)
  local copies, waits for them, and re-layouts  76.9 us (11%)
  starting transfers between devices  16.8 us (2%)
  between operations  15.1 us (2%)
    another operation x24, other arithmetic, tall_cholesky(): pivot_factor = jnp.linalg.cholesky(pivot)  105 us
    another operation x16, other arithmetic, tall_cholesky(): lax.linalg.triangular_solve(pivot_factor, eye, left_side=True, lower=True)  93.2 us
    all_to_all x1, waiting for transfers between devices, per_device(): lax.all_to_all(send_buffer, ('leaf', 'row'), split_axis=0, concat_axis=0,...  88.5 us
    all_gather x1, waiting for transfers between devices, per_device(): first_cols = lax.all_gather(rest_cols, 'col', axis=0, tiled=False)  73.8 us
    all_gather x1, waiting for transfers between devices, per_device(): diagonal_block = lax.all_gather(diag_row, 'row', axis=0, tiled=True)  58.1 us
    all_gather x1, waiting for transfers between devices, per_device(): lax.all_gather(working[0, :, 0, :], 'col', axis=0, tiled=False)  51.3 us
    dot_general x7, matrix products, tall_cholesky(): jnp.dot(solved, solved[:left].T, precision=HIGHEST, preferred_element_typ...  38 us
    unnamed x97, local copies, waits for them, and re-layouts  33.1 us
  transfers between devices with their start and end apart: 6, of which 5 were waited for; matrix products, arithmetic and copies ran while one was open for 50% of the time, Pallas kernels for 0%

profile of v2, /device:TPU:1, one launch (start us, length us, event | category | flops | bytes accessed | tf_op | source)
XLA Modules:
  0.0 681.5 jit_solution(12737110800584824365)
XLA Ops:
  7.2 1.9 copy.159
  9.9 51.3 %all-gather.10.cloned.1.call-done = f32[16,128,1,128]{3,1,2,0:T(8,128)} async-done(((f32[1,128,1,128]{3,1,2,0:T(8,128)}), f32[16,128,1,128]{3,1,2,0:T(8,128)}) %all-gather.10.cloned.1.call-update) | async-done | bytes 1048592 | tf_op jit(solution)/shard_map/all_gather | solution.py:76
  63.3 1.7 slice_bitcast_fusion.3
  65.8 58.1 %all-gather.8.cloned.1.call-done = f32[1024,1024]{0,1:T(8,128)} async-done(((f32[128,1024]{0,1:T(8,128)}), f32[1024,1024]{0,1:T(8,128)}) %all-gather.8.cloned.1.call-update) | async-done | bytes 4194320 | tf_op jit(solution)/shard_map/all_gather | solution.py:78
  126.2 8.8 %all-to-all-start.1 = ((s32[16,1,1]{2,1,0:T(1,128)}), s32[16,1,1]{2,1,0:T(1,128)S(1)}, u32[]{:S(2)}, u32[]{:S(2)}) async-start(s32[16,1,1]{2,1,0:T(1,128)} %copy.131), calls=%async_computation.1 | async-start | bytes 16384 | tf_op jit(solution)/shard_map/all_to_all | solution.py:155
  140.5 11.7 %cholesky.134 = f32[128,128]{1,0:T(8,128)S(1)} custom-call(f32[128,128]{1,0:T(8,128)S(1)} %fusion.60), custom_call_target="Cholesky" | custom-call | tf_op jit(solution)/shard_map/jit(cholesky)/cholesky | solution.py:41
  153.6 9.8 %custom-call.12 = f32[1,128,128]{1,2,0:T(8,128)S(1)} custom-call(f32[1,128,128]{2,1,0:T(8,128)S(1)} %get-tuple-element.34), custom_call_target="InvertDiagBlocksLowerTriangular" | custom-call | tf_op jit(solution)/shard_map/triangular_solve/custom-call.0 | solution.py:42
  165.0 1.8 copy.158
  166.7 73.8 %all-gather.12.cloned.1.call-done = f32[112,128,128]{2,1,0:T(8,128)} async-done(((f32[7,128,128]{2,1,0:T(8,128)}), f32[112,128,128]{2,1,0:T(8,128)}) %all-gather.12.cloned.1.call-update) | async-done | bytes 7340048 | tf_op jit(solution)/shard_map/all_gather | solution.py:82
  240.5 2.0 slice-done
  242.6 2.1 copy.111
  244.6 2.6 copy.157
  247.3 5.2 copy.112
  252.5 3.3 fusion.8
  256.0 6.6 fusion
  262.7 3.2 copy-done.1
  266.8 11.9 %cholesky.145 = f32[128,128]{1,0:T(8,128)S(1)} custom-call(f32[128,128]{1,0:T(8,128)S(1)} %fusion.58), custom_call_target="Cholesky" | custom-call | tf_op jit(solution)/shard_map/jit(cholesky)/cholesky | solution.py:41
  280.0 9.8 %custom-call.13 = f32[1,128,128]{1,2,0:T(8,128)S(1)} custom-call(f32[1,128,128]{2,1,0:T(8,128)S(1)} %get-tuple-element.32), custom_call_target="InvertDiagBlocksLowerTriangular" | custom-call | tf_op jit(solution)/shard_map/triangular_solve/custom-call.0 | solution.py:42
  290.1 3.2 fusion.14
  293.3 8.4 %slice_subtract_fusion = f32[2176,768]{0,1:T(8,128)S(1)} fusion(f32[2304,896]{0,1:T(8,128)} %copy-done.1, f32[2176,128]{1,0:T(8,128)S(1)} %fusion.14), kind=kOutput, calls=%fused_computation.5 | convolution fusion | flops 2568585216 | bytes 14876672 | tf_op jit(solution)/shard_map/dot_general | solution.py:52
  301.7 2.8 copy-done.2
  305.4 11.7 %cholesky.156 = f32[128,128]{1,0:T(8,128)S(1)} custom-call(f32[128,128]{1,0:T(8,128)S(1)} %fusion.56), custom_call_target="Cholesky" | custom-call | tf_op jit(solution)/shard_map/jit(cholesky)/cholesky | solution.py:41
  318.5 9.8 %custom-call.14 = f32[1,128,128]{1,2,0:T(8,128)S(1)} custom-call(f32[1,128,128]{2,1,0:T(8,128)S(1)} %get-tuple-element.30), custom_call_target="InvertDiagBlocksLowerTriangular" | custom-call | tf_op jit(solution)/shard_map/triangular_solve/custom-call.0 | solution.py:42
  328.6 3.0 fusion.16
  331.6 7.0 %slice_subtract_fusion.1 = f32[2048,640]{0,1:T(8,128)S(1)} fusion(f32[2176,768]{0,1:T(8,128)} %copy-done.2, f32[2048,128]{1,0:T(8,128)S(1)} %fusion.16), kind=kOutput, calls=%fused_computation.6 | convolution fusion | flops 2014576640 | bytes 11862016 | tf_op jit(solution)/shard_map/dot_general | solution.py:52
  338.7 2.3 copy-done.3
  342.0 11.7 %cholesky.167 = f32[128,128]{1,0:T(8,128)S(1)} custom-call(f32[128,128]{1,0:T(8,128)S(1)} %fusion.54), custom_call_target="Cholesky" | custom-call | tf_op jit(solution)/shard_map/jit(cholesky)/cholesky | solution.py:41
  355.8 9.8 %custom-call.15 = f32[1,128,128]{1,2,0:T(8,128)S(1)} custom-call(f32[1,128,128]{2,1,0:T(8,128)S(1)} %get-tuple-element.28), custom_call_target="InvertDiagBlocksLowerTriangular" | custom-call | tf_op jit(solution)/shard_map/triangular_solve/custom-call.0 | solution.py:42
  365.9 2.9 fusion.20
  368.8 6.0 slice_subtract_fusion.2
  374.8 1.8 copy-done.5
  379.7 12.7 %cholesky.178 = f32[128,128]{1,0:T(8,128)S(1)} custom-call(f32[128,128]{1,0:T(8,128)} %fusion.52), custom_call_target="Cholesky" | custom-call | tf_op jit(solution)/shard_map/jit(cholesky)/cholesky | solution.py:41
  393.7 2.0 select_bitcast_fusion.3
  395.7 11.3 %custom-call.16 = f32[1,128,128]{1,2,0:T(8,128)} custom-call(f32[1,128,128]{2,1,0:T(8,128)} %get-tuple-element.26), custom_call_target="InvertDiagBlocksLowerTriangular" | custom-call | tf_op jit(solution)/shard_map/triangular_solve/custom-call.0 | solution.py:42
  408.1 2.8 fusion.22
  410.9 4.5 convolution_subtract_fusion
  420.7 13.5 %cholesky.189 = f32[128,128]{1,0:T(8,128)} custom-call(f32[128,128]{1,0:T(8,128)} %fusion.50), custom_call_target="Cholesky" | custom-call | tf_op jit(solution)/shard_map/jit(cholesky)/cholesky | solution.py:41
  435.8 2.1 select_bitcast_fusion.2
  437.8 11.3 %custom-call.17 = f32[1,128,128]{1,2,0:T(8,128)} custom-call(f32[1,128,128]{2,1,0:T(8,128)} %get-tuple-element.24), custom_call_target="InvertDiagBlocksLowerTriangular" | custom-call | tf_op jit(solution)/shard_map/triangular_solve/custom-call.0 | solution.py:42
  450.2 2.7 fusion.24
  452.9 3.3 convolution_subtract_fusion.1
  461.1 13.2 %cholesky.200 = f32[128,128]{1,0:T(8,128)} custom-call(f32[128,128]{1,0:T(8,128)} %fusion.48), custom_call_target="Cholesky" | custom-call | tf_op jit(solution)/shard_map/jit(cholesky)/cholesky | solution.py:41
  475.9 2.2 select_bitcast_fusion.1
  478.1 11.5 %custom-call.18 = f32[1,128,128]{1,2,0:T(8,128)} custom-call(f32[1,128,128]{2,1,0:T(8,128)} %get-tuple-element.22), custom_call_target="InvertDiagBlocksLowerTriangular" | custom-call | tf_op jit(solution)/shard_map/triangular_solve/custom-call.0 | solution.py:42
  490.7 2.5 fusion.26
  493.2 2.3 convolution_subtract_fusion.2
  497.7 11.7 %cholesky.211 = f32[128,128]{1,0:T(8,128)S(1)} custom-call(f32[128,128]{1,0:T(8,128)S(1)} %fusion.46), custom_call_target="Cholesky" | custom-call | tf_op jit(solution)/shard_map/jit(cholesky)/cholesky | solution.py:41
  510.7 9.8 %custom-call.19 = f32[1,128,128]{1,2,0:T(8,128)S(1)} custom-call(f32[1,128,128]{2,1,0:T(8,128)S(1)} %get-tuple-element.20), custom_call_target="InvertDiagBlocksLowerTriangular" | custom-call | tf_op jit(solution)/shard_map/triangular_solve/custom-call.0 | solution.py:42
  521.7 2.2 slice_dynamic-update-slice_fusion.4
  524.8 2.1 slice_dynamic-update-slice_fusion.2
  528.8 2.2 convolution_dynamic-update-slice_fusion
  531.0 2.5 slice.239
  533.6 1.9 slice_select_fusion
  537.7 6.0 fusion.6
  543.8 2.4 copy.129
  546.2 3.7 concatenate.53
  550.1 3.8 convolution_bitcast_fusion
  553.8 6.5 copy.130
  560.3 7.8 %all-to-all-start = ((f32[16,1,65536]{2,1,0:T(1,128)}), f32[16,1,65536]{2,1,0:T(1,128)}, u32[]{:S(2)}, u32[]{:S(2)}) async-start(f32[16,1,65536]{2,1,0:T(1,128)} %copy.130), calls=%async_computation | async-start | bytes 8388608 | tf_op jit(solution)/shard_map/all_to_all | solution.py:154
  569.2 3.5 copy.133
  572.7 88.5 %all-to-all-done = f32[16,1,65536]{2,1,0:T(1,128)} async-done(((f32[16,1,65536]{2,1,0:T(1,128)}), f32[16,1,65536]{2,1,0:T(1,128)}, u32[]{:S(2)}, u32[]{:S(2)}) %all-to-all-start) | async-done | bytes 4194336 | tf_op jit(solution)/shard_map/all_to_all | solution.py:154
  661.1 7.8 %convolution_bitcast_fusion.1 = f32[4,2,65536]{2,0,1:T(4,128)} fusion(f32[16,1,65536]{2,1,0:T(1,128)} %all-to-all-done, s32[2,8]{1,0:T(2,128)S(1)} %eq.153), kind=kOutput, calls=%fused_computation.1 | convolution fusion | flops 50331712 | bytes 6291520 | tf_op jit(solution)/shard_map/slrk,lrkx->slx/dot_general | solution.py:165
  668.9 3.0 reshape.454
  672.0 2.8 fusion.7
  (214 shorter events, 54.5 us)
Async XLA Ops:
  7.2 117.4 %copy-start.40 = (s32[2,56]{1,0:T(2,128)S(1)}, s32[2,56]{1,0:T(2,128)}, u32[]{:S(2)}) copy-start(s32[2,56]{1,0:T(2,128)} %param.9) | copy-start | bytes 1348
  7.2 54.0 %all-gather.10.cloned.1.call-start = ((), (), s32[]{:S(2)}) async-start(), calls=%async_computation.3 | async-start | bytes 1114112 | tf_op jit(solution)/shard_map/all_gather | solution.py:76
  9.1 155.9 %copy-start.12 = (f32[1,8,1,128,4,1,128]{6,3,4,1,5,2,0:T(8,128)}, f32[1,8,1,128,4,1,128]{6,3,4,1,5,2,0:T(8,128)S(1)}, u32[]{:S(2)}) copy-start(f32[1,8,1,128,4,1,128]{6,3,4,1,5,2,0:T(8,128)S(1)} %copy.159) | copy-start | bytes 6291460
  9.8 114.1 %all-gather.8.cloned.1.call-start = ((), (), s32[]{:S(2)}) async-start(), calls=%async_computation.2 | async-start | bytes 4718592 | tf_op jit(solution)/shard_map/all_gather | solution.py:78
  63.2 101.7 %all-gather.14.cloned.1.call-start = ((), (), s32[]{:S(2)}) async-start(), calls=%async_computation.5 | async-start | bytes 2359296 | tf_op jit(solution)/shard_map/all_gather | solution.py:84
  123.9 116.6 %all-gather.12.cloned.1.call-start = ((), (), s32[]{:S(2)}) async-start(), calls=%async_computation.4 | async-start | bytes 7798784 | tf_op jit(solution)/shard_map/all_gather | solution.py:82
  124.5 0.9 copy-start.31
  124.8 0.6 copy-start.29
  125.0 0.6 copy-start.34
  126.2 434.1 %all-to-all-start.1 = ((s32[16,1,1]{2,1,0:T(1,128)}), s32[16,1,1]{2,1,0:T(1,128)S(1)}, u32[]{:S(2)}, u32[]{:S(2)}) async-start(s32[16,1,1]{2,1,0:T(1,128)} %copy.131), calls=%async_computation.1 | async-start | bytes 16384 | tf_op jit(solution)/shard_map/all_to_all | solution.py:155
  138.1 0.6 copy-start.36
  240.5 2.0 slice-start
  252.5 3.3 copy-start
  252.5 3.6 copy-start.4
  256.0 239.5 %copy-start.6 = (f32[2304,128]{1,0:T(8,128)}, f32[2304,128]{1,0:T(8,128)S(1)}, u32[]{:S(2)}) copy-start(f32[2304,128]{1,0:T(8,128)S(1)} %fusion.8) | copy-start | bytes 3538948
  262.6 3.2 copy-start.1
  293.3 227.5 %copy-start.7 = (f32[2176,128]{1,0:T(8,128)}, f32[2176,128]{1,0:T(8,128)S(1)}, u32[]{:S(2)}) copy-start(f32[2176,128]{1,0:T(8,128)S(1)} %fusion.14) | copy-start | bytes 3342340
  301.7 2.8 copy-start.2
  331.6 7.1 %copy-start.8 = (f32[2048,128]{1,0:T(8,128)}, f32[2048,128]{1,0:T(8,128)S(1)}, u32[]{:S(2)}) copy-start(f32[2048,128]{1,0:T(8,128)S(1)} %fusion.16) | copy-start | bytes 3145732
  338.7 2.3 copy-start.3
  368.8 155.1 %copy-start.10 = (f32[1920,128]{1,0:T(8,128)}, f32[1920,128]{1,0:T(8,128)S(1)}, u32[]{:S(2)}) copy-start(f32[1920,128]{1,0:T(8,128)S(1)} %fusion.20) | copy-start | bytes 2949124
  374.8 1.9 copy-start.5
  392.5 0.6 copy-start.23
  410.9 4.6 copy-start.11
  415.5 1.5 copy-start.9
  452.9 3.3 copy-start.14
  456.2 1.2 copy-start.18
  493.2 3.3 copy-start.16
  495.5 1.2 copy-start.19
  496.7 30.2 %copy-start.15 = (f32[1664,128]{1,0:T(8,128)S(1)}, f32[1664,128]{1,0:T(8,128)}, u32[]{:S(2)}) copy-start(f32[1664,128]{1,0:T(8,128)} %copy-done.14) | copy-start | bytes 2555908
  520.5 7.4 %copy-start.17 = (f32[1536,128]{1,0:T(8,128)S(1)}, f32[1536,128]{1,0:T(8,128)}, u32[]{:S(2)}) copy-start(f32[1536,128]{1,0:T(8,128)} %copy-done.16) | copy-start | bytes 2359300
  521.7 7.0 %copy-start.20 = (f32[1536,128]{0,1:T(8,128)S(1)}, f32[1536,128]{0,1:T(8,128)}, u32[]{:S(2)}) copy-start(f32[1536,128]{0,1:T(8,128)} %copy-done.19) | copy-start | bytes 2359300
  531.0 2.5 copy-start.42
  533.5 2.2 slice-start.1
  533.5 2.3 slice-start.2
  533.5 2.3 slice-start.3
  533.5 2.3 copy-start.26
  533.5 2.5 slice-start.4
  533.6 2.5 copy-start.24
  533.6 2.5 copy-start.28
  533.6 3.1 slice-start.5
  533.6 3.1 copy-start.27
  533.6 3.3 slice-start.6
  533.6 3.3 copy-start.25
  535.5 1.6 slice-start.7
  535.6 1.6 copy-start.22
  535.6 1.9 copy-start.38
  535.6 1.9 copy-start.39
  535.6 2.0 copy-start.33
  535.6 2.1 copy-start.13
  543.8 6.2 copy-start.37
  543.8 6.3 copy-start.30
  543.8 6.3 copy-start.32
  543.8 6.3 copy-start.35
  560.3 7.9 %copy-start.41 = (s32[2,56]{1,0:T(2,128)S(1)}, s32[2,56]{1,0:T(2,128)}, u32[]{:S(2)}) copy-start(s32[2,56]{1,0:T(2,128)} %param.9) | copy-start | bytes 1348
  560.3 100.8 %all-to-all-start = ((f32[16,1,65536]{2,1,0:T(1,128)}), f32[16,1,65536]{2,1,0:T(1,128)}, u32[]{:S(2)}, u32[]{:S(2)}) async-start(f32[16,1,65536]{2,1,0:T(1,128)} %copy.130), calls=%async_computation | async-start | bytes 8388608 | tf_op jit(solution)/shard_map/all_to_all | solution.py:154
  572.7 99.3 %copy-start.21 = (f32[4,1,1,128,4,1,128]{6,5,4,3,2,1,0:T(1,128)S(1)}, f32[4,1,1,128,4,1,128]{6,5,4,3,2,1,0:T(1,128)}, u32[]{:S(2)}) copy-start(f32[4,1,1,128,4,1,128]{6,5,4,3,2,1,0:T(1,128)} %param.8) | copy-start | bytes 3145732
Sparse Core Ops, SparseCore 0:
  11.0 50.0 all-gather.9
  63.4 60.4 all-gather.7
  125.7 39.2 all-gather.13
  167.2 73.2 all-gather.11

commit v3 on v2

--- a/solution.py
+++ b/solution.py
@@ -30,10 +30,10 @@
 
 def tall_cholesky(diagonal_block, below_rows):
     size = diagonal_block.shape[0]
-    remaining = jnp.concatenate([diagonal_block, below_rows], axis=0)
+    remaining = diagonal_block
     eye = jnp.eye(TILE, dtype=jnp.float32)
     diag_columns = []
-    below_columns = []
+    inverses = []
     for step in range(size // TILE):
         low = step * TILE
         left = size - low - TILE
@@ -42,20 +42,39 @@
         pivot_inverse = lax.linalg.triangular_solve(
             pivot_factor, eye, left_side=True, lower=True
         )
-        under = remaining[TILE:, :TILE]
-        solved = jnp.dot(
-            under, pivot_inverse.T, precision=HIGHEST, preferred_element_type=jnp.float32
-        )
-        diag_columns.append(jnp.concatenate([jnp.zeros((low, TILE), jnp.float32), pivot_factor, solved[:left]], axis=0))
-        below_columns.append(solved[left:])
+        inverses.append(pivot_inverse)
+        parts = [jnp.zeros((low, TILE), jnp.float32), pivot_factor]
         if left:
+            solved = jnp.dot(
+                remaining[TILE:, :TILE],
+                pivot_inverse.T,
+                precision=HIGHEST,
+                preferred_element_type=jnp.float32,
+            )
+            parts.append(solved)
             update = jnp.dot(
-                solved, solved[:left].T, precision=HIGHEST, preferred_element_type=jnp.float32
+                solved, solved.T, precision=HIGHEST, preferred_element_type=jnp.float32
             )
             remaining = remaining[TILE:, TILE:] - update
+        diag_columns.append(jnp.concatenate(parts, axis=0))
     lower_factor = jnp.concatenate(diag_columns, axis=1)
+    rest = below_rows
+    below_columns = []
+    for step in range(size // TILE):
+        low = step * TILE
+        solved = jnp.dot(
+            rest[:, :TILE], inverses[step].T, precision=HIGHEST, preferred_element_type=jnp.float32
+        )
+        below_columns.append(solved)
+        if low + TILE < size:
+            update = jnp.dot(
+                solved,
+                lower_factor[low + TILE :, low : low + TILE].T,
+                precision=HIGHEST,
+                preferred_element_type=jnp.float32,
+            )
+            rest = rest[:, TILE:] - update
     return lower_factor, jnp.concatenate(below_columns, axis=1)
-
 
 def per_device(front, parent, tile_map, col_shift):
     leaf_count = lax.axis_size("leaf")

time: 692 us -> 568 us (0.82)
  waiting for transfers between devices: 274 us -> 198 us
  local copies, waits for them, and re-layouts: 76.9 us -> 57.1 us
  other arithmetic: 213 us -> 197 us
  matrix products: 85.8 us -> 74.3 us
    all_gather x1, waiting for transfers between devices: 73.8 us -> 0.02 us  [per_device(): first_cols = lax.all_gather(rest_cols, 'col', axis=0, tiled=False)]
    unnamed x97 -> x111, local copies, waits for them, and re-layouts: 33.1 us -> 14.3 us
    dot_general x15 -> x29, matrix products: 60.6 us -> 47.7 us  [the longest x7 21.2 us: tall_cholesky(): jnp.dot(solved, lower_factor[low + TILE:, low:low + TILE].T, precision=HI...]
    div x8, other arithmetic: 8.87 us -> 1.79 us  [tall_cholesky(): pivot_factor = jnp.linalg.cholesky(pivot)]
  transfers between devices with their start and end apart: 6 -> 6, of which waited for: 5 -> 3; matrix products, arithmetic and copies ran while one was open for 50% -> 54% of each run, Pallas kernels for 0% -> 0%
where the time goes in v3:
time: 568 us; the launch traced here: 558 us
  waiting for transfers between devices  198 us (35%)
  other arithmetic  197 us (35%)
  matrix products  74.3 us (13%)
  local copies, waits for them, and re-layouts  57.1 us (10%)
  starting transfers between devices  16.6 us (3%)
  between operations  15.6 us (3%)
    another operation x24, other arithmetic, tall_cholesky(): pivot_factor = jnp.linalg.cholesky(pivot)  99.6 us
    all_to_all x1, waiting for transfers between devices, per_device(): lax.all_to_all(send_buffer, ('leaf', 'row'), split_axis=0, concat_axis=0,...  88.1 us
    another operation x16, other arithmetic, tall_cholesky(): lax.linalg.triangular_solve(pivot_factor, eye, left_side=True, lower=True)  87.2 us
    all_gather x1, waiting for transfers between devices, per_device(): diagonal_block = lax.all_gather(diag_row, 'row', axis=0, tiled=True)  58.1 us
    all_gather x1, waiting for transfers between devices, per_device(): lax.all_gather(working[0, :, 0, :], 'col', axis=0, tiled=False)  51.3 us
    dot_general x7, matrix products, tall_cholesky(): jnp.dot(solved, lower_factor[low + TILE:, low:low + TILE].T, precision=HI...  21.2 us
    unnamed x111, local copies, waits for them, and re-layouts  14.3 us
    dot_general x7, matrix products, tall_cholesky(): jnp.dot(solved, solved.T, precision=HIGHEST, preferred_element_type=jnp.f...  12.8 us
  transfers between devices with their start and end apart: 6, of which 3 were waited for; matrix products, arithmetic and copies ran while one was open for 54% of the time, Pallas kernels for 0%

profile of v3, /device:TPU:1, one launch (start us, length us, event | category | flops | bytes accessed | tf_op | source)
XLA Modules:
  0.0 557.9 jit_solution(11037079520208860323)
XLA Ops:
  7.2 1.9 copy.164
  9.9 51.3 %all-gather.10.cloned.1.call-done = f32[16,128,1,128]{3,1,2,0:T(8,128)} async-done(((f32[1,128,1,128]{3,1,2,0:T(8,128)}), f32[16,128,1,128]{3,1,2,0:T(8,128)}) %all-gather.10.cloned.1.call-update) | async-done | bytes 1048592 | tf_op jit(solution)/shard_map/all_gather | solution.py:95
  61.1 1.1 slice_bitcast_fusion.1
  62.2 1.0 copy.115
  63.3 1.7 slice_bitcast_fusion.3
  65.8 58.1 %all-gather.8.cloned.1.call-done = f32[1024,1024]{0,1:T(8,128)} async-done(((f32[128,1024]{0,1:T(8,128)}), f32[1024,1024]{0,1:T(8,128)}) %all-gather.8.cloned.1.call-update) | async-done | bytes 4194320 | tf_op jit(solution)/shard_map/all_gather | solution.py:97
  125.8 8.8 %all-to-all-start.1 = ((s32[16,1,1]{2,1,0:T(1,128)}), s32[16,1,1]{2,1,0:T(1,128)S(1)}, u32[]{:S(2)}, u32[]{:S(2)}) async-start(s32[16,1,1]{2,1,0:T(1,128)} %copy.138), calls=%async_computation.1 | async-start | bytes 16384 | tf_op jit(solution)/shard_map/all_to_all | solution.py:174
  139.9 11.7 %cholesky.134 = f32[128,128]{1,0:T(8,128)S(1)} custom-call(f32[128,128]{1,0:T(8,128)S(1)} %fusion.68), custom_call_target="Cholesky" | custom-call | tf_op jit(solution)/shard_map/jit(cholesky)/cholesky | solution.py:41
  152.3 1.3 select_bitcast_fusion.7
  153.6 9.8 %custom-call.12 = f32[1,128,128]{1,2,0:T(8,128)S(1)} custom-call(f32[1,128,128]{2,1,0:T(8,128)S(1)} %get-tuple-element.34), custom_call_target="InvertDiagBlocksLowerTriangular" | custom-call | tf_op jit(solution)/shard_map/triangular_solve/custom-call.0 | solution.py:42
  164.3 1.9 fusion.23
  167.0 4.6 slice_subtract_fusion.2
  171.7 12.0 %cholesky.145 = f32[128,128]{1,0:T(8,128)S(1)} custom-call(f32[128,128]{1,0:T(8,128)S(1)} %fusion.66), custom_call_target="Cholesky" | custom-call | tf_op jit(solution)/shard_map/jit(cholesky)/cholesky | solution.py:41
  184.4 1.3 select_bitcast_fusion.6
  185.7 9.8 %custom-call.13 = f32[1,128,128]{1,2,0:T(8,128)S(1)} custom-call(f32[1,128,128]{2,1,0:T(8,128)S(1)} %get-tuple-element.32), custom_call_target="InvertDiagBlocksLowerTriangular" | custom-call | tf_op jit(solution)/shard_map/triangular_solve/custom-call.0 | solution.py:42
  197.3 2.0 slice_subtract_fusion.3
  199.3 1.5 copy-done.5
  201.7 11.7 %cholesky.156 = f32[128,128]{1,0:T(8,128)S(1)} custom-call(f32[128,128]{1,0:T(8,128)S(1)} %fusion.64), custom_call_target="Cholesky" | custom-call | tf_op jit(solution)/shard_map/jit(cholesky)/cholesky | solution.py:41
  214.1 1.3 select_bitcast_fusion.5
  215.4 10.0 %custom-call.14 = f32[1,128,128]{1,2,0:T(8,128)S(1)} custom-call(f32[1,128,128]{2,1,0:T(8,128)S(1)} %get-tuple-element.30), custom_call_target="InvertDiagBlocksLowerTriangular" | custom-call | tf_op jit(solution)/shard_map/triangular_solve/custom-call.0 | solution.py:42
  226.3 1.7 fusion.27
  228.0 2.9 slice_subtract_fusion.4
  231.0 11.7 %cholesky.167 = f32[128,128]{1,0:T(8,128)S(1)} custom-call(f32[128,128]{1,0:T(8,128)S(1)} %fusion.62), custom_call_target="Cholesky" | custom-call | tf_op jit(solution)/shard_map/jit(cholesky)/cholesky | solution.py:41
  243.4 1.3 select_bitcast_fusion.4
  244.7 9.8 %custom-call.15 = f32[1,128,128]{1,2,0:T(8,128)S(1)} custom-call(f32[1,128,128]{2,1,0:T(8,128)S(1)} %get-tuple-element.28), custom_call_target="InvertDiagBlocksLowerTriangular" | custom-call | tf_op jit(solution)/shard_map/triangular_solve/custom-call.0 | solution.py:42
  256.0 1.0 convolution_subtract_fusion.5
  257.2 11.9 %cholesky.178 = f32[128,128]{1,0:T(8,128)S(1)} custom-call(f32[128,128]{1,0:T(8,128)S(1)} %fusion.60), custom_call_target="Cholesky" | custom-call | tf_op jit(solution)/shard_map/jit(cholesky)/cholesky | solution.py:41
  269.8 1.3 select_bitcast_fusion.3
  271.1 9.8 %custom-call.16 = f32[1,128,128]{1,2,0:T(8,128)S(1)} custom-call(f32[1,128,128]{2,1,0:T(8,128)S(1)} %get-tuple-element.26), custom_call_target="InvertDiagBlocksLowerTriangular" | custom-call | tf_op jit(solution)/shard_map/triangular_solve/custom-call.0 | solution.py:42
  282.5 11.7 %cholesky.189 = f32[128,128]{1,0:T(8,128)S(1)} custom-call(f32[128,128]{1,0:T(8,128)S(1)} %fusion.58), custom_call_target="Cholesky" | custom-call | tf_op jit(solution)/shard_map/jit(cholesky)/cholesky | solution.py:41
  295.6 9.8 %custom-call.17 = f32[1,128,128]{1,2,0:T(8,128)S(1)} custom-call(f32[1,128,128]{2,1,0:T(8,128)S(1)} %get-tuple-element.24), custom_call_target="InvertDiagBlocksLowerTriangular" | custom-call | tf_op jit(solution)/shard_map/triangular_solve/custom-call.0 | solution.py:42
  306.2 1.3 fusion.49
  307.5 1.4 convolution_subtract_fusion.7
  309.0 11.7 %cholesky.200 = f32[128,128]{1,0:T(8,128)S(1)} custom-call(f32[128,128]{1,0:T(8,128)S(1)} %fusion.56), custom_call_target="Cholesky" | custom-call | tf_op jit(solution)/shard_map/jit(cholesky)/cholesky | solution.py:41
  322.1 9.8 %custom-call.18 = f32[1,128,128]{1,2,0:T(8,128)S(1)} custom-call(f32[1,128,128]{2,1,0:T(8,128)S(1)} %get-tuple-element.22), custom_call_target="InvertDiagBlocksLowerTriangular" | custom-call | tf_op jit(solution)/shard_map/triangular_solve/custom-call.0 | solution.py:42
  332.9 11.7 %cholesky.211 = f32[128,128]{1,0:T(8,128)S(1)} custom-call(f32[128,128]{1,0:T(8,128)S(1)} %fusion.54), custom_call_target="Cholesky" | custom-call | tf_op jit(solution)/shard_map/jit(cholesky)/cholesky | solution.py:41
  345.9 10.0 %custom-call.19 = f32[1,128,128]{1,2,0:T(8,128)S(1)} custom-call(f32[1,128,128]{2,1,0:T(8,128)S(1)} %get-tuple-element.20), custom_call_target="InvertDiagBlocksLowerTriangular" | custom-call | tf_op jit(solution)/shard_map/triangular_solve/custom-call.0 | solution.py:42
  360.8 2.3 copy.132
  363.2 2.0 slice-done
  365.2 2.1 copy.131
  369.8 5.4 slice_subtract_fusion
  376.1 3.8 slice_subtract_fusion.1
  380.7 3.9 convolution_subtract_fusion
  385.5 3.0 convolution_subtract_fusion.1
  389.4 2.5 convolution_subtract_fusion.2
  392.8 1.3 convolution_subtract_fusion.3
  395.0 1.3 convolution_subtract_fusion.4
  397.1 2.5 copy-done.6
  399.6 2.1 slice.222
  401.8 5.1 copy.133
  406.8 1.0 constant_dynamic-slice_fusion
  407.9 1.8 slice_select_fusion
  409.7 1.8 copy.152
  411.6 8.9 %fusion.5 = f32[7,128,4,128]{3,1,2,0:T(8,128)S(1)} fusion(f32[1,8,1,128,4,1,128]{6,3,4,1,5,2,0:T(8,128)} %copy-done.4, f32[7,128,1024,1]{2,1,3,0:T(8,128)} %bitcast.198, f32[4,128,1024,1]{2,1,0,3:T(8,128)} %bitcast.203, f32[7,128,128]{2,1,0:T(8,128)S(1)} %constant_dynamic-slice_fusion, pred[4]{0:T(512)(128)(4,1)S(1)} %copy-done.44), kind=kOutput, calls=%fused_computation.23 | convolution fusion | flops 5638062080 | bytes 9895940 | tf_op jit(solution)/shard_map/atk,bsk->atbs/dot_general | solution.py:115
  420.6 2.4 copy.136
  423.0 3.7 concatenate.53
  426.8 3.8 convolution_bitcast_fusion
  430.6 6.3 %copy.137 = f32[16,1,65536]{2,1,0:T(1,128)} copy(f32[16,1,65536]{2,0,1:T(8,128)S(1)} %convolution_bitcast_fusion) | data formatting | bytes 8388608 | tf_op jit(solution)/shard_map/oka,ax->okx/dot_general | solution.py:163
  436.9 7.6 %all-to-all-start = ((f32[16,1,65536]{2,1,0:T(1,128)}), f32[16,1,65536]{2,1,0:T(1,128)}, u32[]{:S(2)}, u32[]{:S(2)}) async-start(f32[16,1,65536]{2,1,0:T(1,128)} %copy.137), calls=%async_computation | async-start | bytes 8388608 | tf_op jit(solution)/shard_map/all_to_all | solution.py:173
  445.6 3.5 copy.140
  449.1 88.1 %all-to-all-done = f32[16,1,65536]{2,1,0:T(1,128)} async-done(((f32[16,1,65536]{2,1,0:T(1,128)}), f32[16,1,65536]{2,1,0:T(1,128)}, u32[]{:S(2)}, u32[]{:S(2)}) %all-to-all-start) | async-done | bytes 4194336 | tf_op jit(solution)/shard_map/all_to_all | solution.py:173
  537.2 7.8 %convolution_bitcast_fusion.1 = f32[4,2,65536]{2,0,1:T(4,128)} fusion(f32[16,1,65536]{2,1,0:T(1,128)} %all-to-all-done, s32[2,8]{1,0:T(2,128)S(1)} %eq.153), kind=kOutput, calls=%fused_computation.1 | convolution fusion | flops 50331712 | bytes 6291520 | tf_op jit(solution)/shard_map/slrk,lrkx->slx/dot_general | solution.py:184
  545.0 3.1 reshape.454
  548.1 2.8 fusion.6
  (230 shorter events, 40.7 us)
Async XLA Ops:
  7.2 116.8 %copy-start.51 = (s32[2,56]{1,0:T(2,128)S(1)}, s32[2,56]{1,0:T(2,128)}, u32[]{:S(2)}) copy-start(s32[2,56]{1,0:T(2,128)} %param.9) | copy-start | bytes 1348
  7.2 54.0 %all-gather.10.cloned.1.call-start = ((), (), s32[]{:S(2)}) async-start(), calls=%async_computation.3 | async-start | bytes 1114112 | tf_op jit(solution)/shard_map/all_gather | solution.py:95
  9.1 154.6 %copy-start.4 = (f32[1,8,1,128,4,1,128]{6,3,4,1,5,2,0:T(8,128)}, f32[1,8,1,128,4,1,128]{6,3,4,1,5,2,0:T(8,128)S(1)}, u32[]{:S(2)}) copy-start(f32[1,8,1,128,4,1,128]{6,3,4,1,5,2,0:T(8,128)S(1)} %copy.164) | copy-start | bytes 6291460
  9.8 114.1 %all-gather.8.cloned.1.call-start = ((), (), s32[]{:S(2)}) async-start(), calls=%async_computation.2 | async-start | bytes 4718592 | tf_op jit(solution)/shard_map/all_gather | solution.py:97
  63.2 297.6 %all-gather.14.cloned.1.call-start = ((), (), s32[]{:S(2)}) async-start(), calls=%async_computation.5 | async-start | bytes 2359296 | tf_op jit(solution)/shard_map/all_gather | solution.py:103
  123.9 239.2 %all-gather.12.cloned.1.call-start = ((), (), s32[]{:S(2)}) async-start(), calls=%async_computation.4 | async-start | bytes 7798784 | tf_op jit(solution)/shard_map/all_gather | solution.py:101
  124.0 0.6 copy-start.41
  124.2 0.5 copy-start.39
  124.4 0.5 copy-start.45
  125.8 311.2 %all-to-all-start.1 = ((s32[16,1,1]{2,1,0:T(1,128)}), s32[16,1,1]{2,1,0:T(1,128)S(1)}, u32[]{:S(2)}, u32[]{:S(2)}) async-start(s32[16,1,1]{2,1,0:T(1,128)} %copy.138), calls=%async_computation.1 | async-start | bytes 16384 | tf_op jit(solution)/shard_map/all_to_all | solution.py:174
  137.4 0.7 copy-start.47
  163.7 0.6 copy-start.30
  166.2 0.8 copy-start
  195.8 0.6 copy-start.26
  197.3 2.1 copy-start.2
  199.3 1.5 copy-start.5
  225.7 0.6 copy-start.28
  254.8 0.6 copy-start.16
  257.0 98.9 %copy-start.1 = (f32[896,128]{1,0:T(8,128)S(1)}, f32[896,128]{1,0:T(8,128)}, u32[]{:S(2)}) copy-start(f32[896,128]{1,0:T(8,128)} %copy-done) | copy-start | bytes 1376260
  269.8 87.1 %copy-start.3 = (f32[768,128]{1,0:T(8,128)S(1)}, f32[768,128]{1,0:T(8,128)}, u32[]{:S(2)}) copy-start(f32[768,128]{1,0:T(8,128)} %copy-done.2) | copy-start | bytes 1179652
  281.2 76.5 %copy-start.18 = (f32[128,128]{1,0:T(8,128)}, f32[128,128]{1,0:T(8,128)S(1)}, u32[]{:S(2)}) copy-start(f32[128,128]{1,0:T(8,128)S(1)} %fusion.37) | copy-start | bytes 196612
  281.7 76.5 %copy-start.7 = (f32[384,128]{1,0:T(8,128)}, f32[384,128]{1,0:T(8,128)S(1)}, u32[]{:S(2)}) copy-start(f32[384,128]{1,0:T(8,128)S(1)} %fusion.47) | copy-start | bytes 589828
  282.4 23.1 %copy-start.11 = (f32[384,384]{0,1:T(8,128)}, f32[384,384]{0,1:T(8,128)S(1)}, u32[]{:S(2)}) copy-start(f32[384,384]{0,1:T(8,128)S(1)} %convolution_subtract_fusion.6) | copy-start | bytes 1769476
  282.4 75.4 %copy-start.32 = (f32[128,128]{1,0:T(8,128)S(1)}, f32[128,128]{1,0:T(8,128)}, u32[]{:S(2)}) copy-start(f32[128,128]{1,0:T(8,128)} %get-tuple-element.31) | copy-start | bytes 196612
  282.4 75.4 %copy-start.36 = (f32[1024]{0:T(1024)S(1)}, f32[1024]{0:T(1024)}, u32[]{:S(2)}) copy-start(f32[1024]{0:T(1024)} %pad.10.clone) | copy-start | bytes 12292
  282.4 75.6 %copy-start.35 = (f32[128,128]{1,0:T(8,128)S(1)}, f32[128,128]{1,0:T(8,128)}, u32[]{:S(2)}) copy-start(f32[128,128]{1,0:T(8,128)} %get-tuple-element.29) | copy-start | bytes 196612
  282.4 75.6 %copy-start.38 = (f32[1024]{0:T(1024)S(1)}, f32[1024]{0:T(1024)}, u32[]{:S(2)}) copy-start(f32[1024]{0:T(1024)} %pad.13.clone) | copy-start | bytes 12292
  294.3 63.9 %copy-start.33 = (f32[128,128]{1,0:T(8,128)S(1)}, f32[128,128]{1,0:T(8,128)}, u32[]{:S(2)}) copy-start(f32[128,128]{1,0:T(8,128)} %get-tuple-element.27) | copy-start | bytes 196612
  294.3 63.9 %copy-start.37 = (f32[1024]{0:T(1024)S(1)}, f32[1024]{0:T(1024)}, u32[]{:S(2)}) copy-start(f32[1024]{0:T(1024)} %pad.16.clone) | copy-start | bytes 12292
  306.1 52.3 %copy-start.20 = (f32[128,128]{1,0:T(8,128)}, f32[128,128]{1,0:T(8,128)S(1)}, u32[]{:S(2)}) copy-start(f32[128,128]{1,0:T(8,128)S(1)} %fusion.35) | copy-start | bytes 196612
  307.5 51.0 %copy-start.9 = (f32[256,128]{1,0:T(8,128)}, f32[256,128]{1,0:T(8,128)S(1)}, u32[]{:S(2)}) copy-start(f32[256,128]{1,0:T(8,128)S(1)} %fusion.49) | copy-start | bytes 393220
  332.2 26.8 %copy-start.24 = (f32[128,128]{1,0:T(8,128)}, f32[128,128]{1,0:T(8,128)S(1)}, u32[]{:S(2)}) copy-start(f32[128,128]{1,0:T(8,128)S(1)} %fusion.33) | copy-start | bytes 196612
  332.5 26.5 %copy-start.12 = (f32[128,128]{1,0:T(8,128)}, f32[128,128]{1,0:T(8,128)S(1)}, u32[]{:S(2)}) copy-start(f32[128,128]{1,0:T(8,128)S(1)} %fusion.51) | copy-start | bytes 196612
  332.7 26.2 %copy-start.49 = (s32[128]{0:T(128)S(1)}, s32[128]{0:T(128)}, u32[]{:S(2)}) copy-start(s32[128]{0:T(128)} %get-tuple-element.56) | copy-start | bytes 1540
  332.8 26.2 %copy-start.50 = (s32[128]{0:T(128)S(1)}, s32[128]{0:T(128)}, u32[]{:S(2)}) copy-start(s32[128]{0:T(128)} %get-tuple-element.57) | copy-start | bytes 1540
  332.9 27.1 %copy-start.43 = (pred[4]{0:T(512)(128)(4,1)S(1)}, pred[4]{0:T(512)(128)(4,1)}, u32[]{:S(2)}) copy-start(pred[4]{0:T(512)(128)(4,1)} %get-tuple-element.55) | copy-start | bytes 16
  359.1 1.7 copy-start.22
  363.2 2.0 slice-start
  368.2 0.8 copy-start.31
  369.8 5.4 copy-start.27
  376.1 3.8 copy-start.29
  380.7 4.0 copy-start.17
  385.5 3.0 copy-start.19
  385.5 3.9 copy-start.8
  388.5 3.4 copy-start.21
  389.4 3.4 copy-start.10
  391.9 2.2 copy-start.25
  391.9 3.0 copy-start.13
  392.8 3.5 copy-start.34
  397.1 2.5 copy-start.6
  401.8 6.1 %copy-start.53 = (pred[512]{0:T(512)(128)(4,1)S(1)}, pred[512]{0:T(512)(128)(4,1)}, u32[]{:S(2)}) copy-start(pred[512]{0:T(512)(128)(4,1)} %broadcast_bitcast_fusion) | copy-start | bytes 1540
  407.9 3.7 copy-start.44
  420.5 6.2 %copy-start.48 = (pred[4]{0:T(512)(128)(4,1)S(1)}, pred[4]{0:T(512)(128)(4,1)}, u32[]{:S(2)}) copy-start(pred[4]{0:T(512)(128)(4,1)} %copy-done.47) | copy-start | bytes 16
  420.5 6.3 %copy-start.15 = (f32[128,4,128]{2,1,0:T(4,128)S(1)}, f32[128,4,128]{2,1,0:T(4,128)}, u32[]{:S(2)}) copy-start(f32[128,4,128]{2,1,0:T(4,128)} %broadcast_select_fusion) | copy-start | bytes 786436
  420.5 6.3 %copy-start.40 = (s32[8]{0:T(128)S(1)}, s32[8]{0:T(128)}, u32[]{:S(2)}) copy-start(s32[8]{0:T(128)} %copy-done.39) | copy-start | bytes 100
  420.5 6.3 %copy-start.42 = (pred[8]{0:T(512)(128)(4,1)S(1)}, pred[8]{0:T(512)(128)(4,1)}, u32[]{:S(2)}) copy-start(pred[8]{0:T(512)(128)(4,1)} %copy-done.41) | copy-start | bytes 28
  420.6 6.3 %copy-start.46 = (pred[8]{0:T(512)(128)(4,1)S(1)}, pred[8]{0:T(512)(128)(4,1)}, u32[]{:S(2)}) copy-start(pred[8]{0:T(512)(128)(4,1)} %copy-done.45) | copy-start | bytes 28
  436.9 7.7 %copy-start.52 = (s32[2,56]{1,0:T(2,128)S(1)}, s32[2,56]{1,0:T(2,128)}, u32[]{:S(2)}) copy-start(s32[2,56]{1,0:T(2,128)} %param.9) | copy-start | bytes 1348
  436.9 8.4 %copy-start.23 = (f32[128,128]{1,0:T(8,128)S(1)}, f32[128,128]{1,0:T(8,128)}, u32[]{:S(2)}) copy-start(f32[128,128]{1,0:T(8,128)} %copy-done.22) | copy-start | bytes 196612
  436.9 100.2 %all-to-all-start = ((f32[16,1,65536]{2,1,0:T(1,128)}), f32[16,1,65536]{2,1,0:T(1,128)}, u32[]{:S(2)}, u32[]{:S(2)}) async-start(f32[16,1,65536]{2,1,0:T(1,128)} %copy.137), calls=%async_computation | async-start | bytes 8388608 | tf_op jit(solution)/shard_map/all_to_all | solution.py:173
  545.0 3.1 copy-start.14
Sparse Core Ops, SparseCore 0:
  11.0 50.0 all-gather.9
  63.4 60.4 all-gather.7
  125.7 38.9 all-gather.13
  167.0 73.5 all-gather.11
